TPU v7x, 128 devices: a whole 4x4x4 slice. The times are simulated.
128 devices in a mesh: lat: 8 (over y_lo, z), lon: 16 (over x, y_hi, core).
Axes of the slice: x: 4, y: 4 (y_hi: 2, y_lo: 2; y = y_hi * 2 + y_lo), z: 4, core: 2. Of those that a mesh axis runs over, the one named last changes fastest.
Arguments:
- starting_sea_elevation: float32 [256, 2048], P('lat', 'lon'), may hold values from -6 to 6
- zonal_integrated_flux: float32 [256, 2048], P('lat', 'lon'), may hold values from -6 to 6
- meridional_integrated_flux: float32 [256, 2048], P('lat', 'lon'), may hold values from -6 to 6
- ocean_strata_total: int32 [256, 2048], P('lat', 'lon'), may hold values from 0 to 8
- thermal_anomaly: float32 [8, 256, 2048], P(None, 'lat', 'lon'), may hold values from -6 to 6
- zonal_baroclinic_velocity: float32 [8, 256, 2048], P(None, 'lat', 'lon'), may hold values from -3 to 3
- meridional_baroclinic_velocity: float32 [8, 256, 2048], P(None, 'lat', 'lon'), may hold values from -3 to 3
- sent_sender_mesh_index: int32 [128, 128, 1024], P(('lat', 'lon')), may hold values from 0 to 4095
- sent_intersection_extent: float32 [128, 128, 1024], P(('lat', 'lon')), may hold values from 0.2 to 1
- sent_entry_tally: int32 [128, 128], P(('lat', 'lon')), may hold values from 0 to 1024, as said below
- received_atmosphere_mesh_index: int32 [128, 128, 1024], P(('lat', 'lon')), may hold values from 0 to 4095
Outputs:
- height_new: float32 [256, 2048], P('lat', 'lon')
- east_new: float32 [256, 2048], P('lat', 'lon')
- north_new: float32 [256, 2048], P('lat', 'lon')
- temperature_new: float32 [8, 256, 2048], P(None, 'lat', 'lon')
- atmosphere_fields: float32 [4, 524288], P(None, ('lat', 'lon'))
Inputs may be any that keep to these rules, and one draw needn't show every extreme that they name: Slots j >= sent_entry_tally[s, d] are unused. In every draw one owner receives exactly 1024 live slots from every device. `sent_sender_mesh_index`: A cell of the sending device's block, numbered row by row. `received_atmosphere_mesh_index`: an atmosphere cell of the receiving owner. `ocean_strata_total`: 0 is land.
All inputs are finite; a program needn't handle non-finite values.
Results may differ from a plain program's by a relative error of at most 0.00017.
Values sent between devices are 32-bit elements; how exact they have to be, the bound alone decides.
No kernel may reach another device: no remote copies, remote signals or barrier semaphores. Data moves between devices by JAX's collectives and lax.ppermute only.
A program may use at most 64 MiB of HBM per device.

v0:
```python
import math

import jax
import jax.numpy as jnp
from jax import lax
from jax.experimental import pallas as pl
from jax.sharding import PartitionSpec as P

VERTICAL_STRATA = 8
STEPS = 4
NF = 4
ACELL = 4096


mass_coef = 0.7
slope_coef = 0.7
spin_coef = 0.3
mix_coef = 0.1
carry_coef = 0.1


HALO = 2 * STEPS


def exchange(block, signs, width):
    planes, rows, columns = block.shape
    sectors = lax.axis_size("lon")
    bands = lax.axis_size("lat")
    eastward = [(i, (i + 1) % sectors) for i in range(sectors)]
    westward = [((i + 1) % sectors, i) for i in range(sectors)]
    from_west = lax.ppermute(block[:, :, columns - width :], "lon", eastward)
    from_east = lax.ppermute(block[:, :, :width], "lon", westward)
    wide = jnp.concatenate([from_west, block, from_east], axis=2)
    upward = [(b, b + 1) for b in range(bands - 1)]
    downward = [(b + 1, b) for b in range(bands - 1)]
    top = wide[:, rows - width :, :]
    from_south = lax.ppermute(top, "lat", upward)
    from_north = lax.ppermute(wide[:, :width, :], "lat", downward)
    last = (bands - 1) * sectors
    mirror = [(last + j, last + sectors - 1 - j) for j in range(sectors)]
    folded = lax.ppermute(top, ("lat", "lon"), mirror)
    folded = jnp.flip(folded, axis=(1, 2)) * signs[:, None, None]
    on_top = lax.axis_index("lat") == bands - 1
    north_rim = jnp.where(on_top, folded, from_north)
    return jnp.concatenate([from_south, wide, north_rim], axis=1)


def east_of(x):
    return jnp.concatenate([x[..., 1:], x[..., -1:]], axis=-1)


def west_of(x):
    return jnp.concatenate([x[..., :1], x[..., :-1]], axis=-1)


def north_of(x):
    return jnp.concatenate([x[..., 1:, :], x[..., -1:, :]], axis=-2)


def south_of(x):
    return jnp.concatenate([x[..., :1, :], x[..., :-1, :]], axis=-2)


GROUP = 32
CHUNKS = 2


def split_pieces(x):
    high = x.astype(jnp.bfloat16)
    low = (x - high.astype(jnp.float32)).astype(jnp.bfloat16)
    return high, low


def pick_kernel(table_ref, index_ref, extent_ref, tally_ref, out_ref):
    fields_count = out_ref.shape[1]
    slots = index_ref.shape[1]
    table_rows = table_ref.shape[0]
    columns = table_ref.shape[1]
    rows = table_rows // fields_count
    table = jnp.concatenate(split_pieces(table_ref[...]), axis=1)
    column_ids = lax.broadcasted_iota(jnp.int32, (columns, slots), 0)
    row_ids = lax.broadcasted_iota(jnp.int32, (8, slots), 0)
    slot_ids = lax.broadcasted_iota(jnp.int32, (1, slots), 1)
    for owner in range(index_ref.shape[0]):
        index = index_ref[pl.ds(owner, 1), :]
        hot = (column_ids == index % columns).astype(jnp.bfloat16)
        by_column = jnp.dot(
            table, jnp.concatenate([hot, hot], axis=0), preferred_element_type=jnp.float32
        )
        row = index // columns
        masks = [row_ids + 8 * tile == row for tile in range(rows // 8)]
        weight = jnp.where(
            slot_ids < tally_ref[pl.ds(owner, 1), :], extent_ref[pl.ds(owner, 1), :], 0.0
        )
        for field in range(fields_count):
            chosen = jnp.zeros((8, slots), jnp.float32)
            for tile in range(rows // 8):
                start = field * rows + tile * 8
                chosen = jnp.where(masks[tile], by_column[start : start + 8], chosen)
            picked = jnp.sum(chosen, axis=0, keepdims=True)
            out_ref[owner, pl.ds(field, 1), :] = picked * weight


def pick_cells(surface_grid, indices, extent, tally):
    fields_count, rows, columns = surface_grid.shape
    owners, slots = indices.shape
    table = surface_grid.reshape(fields_count * rows, columns)
    return pl.pallas_call(
        pick_kernel,
        out_shape=jax.ShapeDtypeStruct((owners, fields_count, slots), jnp.float32),
        grid=(owners // GROUP,),
        in_specs=[
            pl.BlockSpec((fields_count * rows, columns), lambda i: (0, 0)),
            pl.BlockSpec((GROUP, slots), lambda i: (i, 0)),
            pl.BlockSpec((GROUP, slots), lambda i: (i, 0)),
            pl.BlockSpec((GROUP, 1), lambda i: (i, 0)),
        ],
        out_specs=pl.BlockSpec((GROUP, fields_count, slots), lambda i: (i, 0, 0)),
    )(table, indices, extent, tally[:, None])


def spread_kernel(value_ref, target_ref, out_ref):
    fields_count = value_ref.shape[1]
    slots = value_ref.shape[2]
    lows = out_ref.shape[0]
    highs = out_ref.shape[1] // (2 * fields_count)

    @pl.when(pl.program_id(0) == 0)
    def _():
        out_ref[...] = jnp.zeros_like(out_ref)

    high_ids = lax.broadcasted_iota(jnp.int32, (highs, slots), 0)
    low_ids = lax.broadcasted_iota(jnp.int32, (lows, slots), 0)
    total = jnp.zeros(out_ref.shape, jnp.float32)
    for sender in range(target_ref.shape[0]):
        target = target_ref[pl.ds(sender, 1), :]
        high_hot = high_ids == target // lows
        low_hot = (low_ids == target % lows).astype(jnp.bfloat16)
        pieces = []
        for field in range(fields_count):
            high, low_part = split_pieces(value_ref[sender, pl.ds(field, 1), :])
            pieces.append((high, low_part))
        weighted = jnp.concatenate(
            [
                jnp.where(high_hot, pieces[field][part].astype(jnp.float32), 0.0).astype(jnp.bfloat16)
                for part in range(2)
                for field in range(fields_count)
            ],
            axis=0,
        )
        total = total + lax.dot_general(
            low_hot, weighted, (((1,), (1,)), ((), ())), preferred_element_type=jnp.float32
        )
    out_ref[...] += total


def spread_cells(values, targets, cells):
    senders, fields_count, slots = values.shape
    lows = 128
    highs = cells // lows
    summed = pl.pallas_call(
        spread_kernel,
        out_shape=jax.ShapeDtypeStruct((lows, 2 * fields_count * highs), jnp.float32),
        grid=(senders // GROUP,),
        in_specs=[
            pl.BlockSpec((GROUP, fields_count, slots), lambda i: (i, 0, 0)),
            pl.BlockSpec((GROUP, slots), lambda i: (i, 0)),
        ],
        out_specs=pl.BlockSpec((lows, 2 * fields_count * highs), lambda i: (0, 0)),
    )(values, targets)
    summed = summed.reshape(lows, 2, fields_count, highs).sum(axis=1)
    return jnp.transpose(summed, (1, 2, 0)).reshape(fields_count, cells)


def local(
    starting_sea_elevation,
    zonal_integrated_flux,
    meridional_integrated_flux,
    ocean_strata_total,
    thermal_anomaly,
    zonal_baroclinic_velocity,
    meridional_baroclinic_velocity,
    sent_sender_mesh_index,
    sent_intersection_extent,
    sent_entry_tally,
    received_atmosphere_mesh_index,
):
    band_rows, band_columns = starting_sea_elevation.shape
    grid_rows = band_rows * lax.axis_size("lat")
    band = lax.axis_index("lat")
    depth = ocean_strata_total.astype(jnp.float32)
    planes = jnp.concatenate(
        [
            jnp.stack([starting_sea_elevation, zonal_integrated_flux, meridional_integrated_flux, depth]),
            thermal_anomaly,
        ],
        axis=0,
    )
    signs = jnp.array([1.0, -1.0, -1.0] + [1.0] * (1 + VERTICAL_STRATA), jnp.float32)
    ext = exchange(planes, signs, HALO)
    depth_ext = ext[3]
    wet = (depth_ext > 0).astype(jnp.float32)
    hnorm = depth_ext / VERTICAL_STRATA
    height = ext[0] * wet
    east = ext[1] * wet
    north = ext[2] * wet
    global_rows = band * band_rows - HALO + jnp.arange(band_rows + 2 * HALO)
    global_rows = jnp.where(global_rows >= grid_rows, 2 * grid_rows - 1 - global_rows, global_rows)
    rows = global_rows.astype(jnp.float32)
    rotation = (-spin_coef * jnp.cos(jnp.pi * (rows + 0.5) / grid_rows))[:, None]
    for step in range(STEPS):
        height = wet * (height - mass_coef * (east_of(east) - west_of(east) + (north_of(north) - south_of(north))))
        east = wet * (east - slope_coef * hnorm * (east_of(height) - west_of(height)) + rotation * north)
        north = wet * (north - slope_coef * hnorm * (north_of(height) - south_of(height)) - rotation * east)
    inner = (slice(HALO, HALO + band_rows), slice(HALO, HALO + band_columns))
    height = height[inner]
    east = east[inner]
    north = north[inner]
    near = (slice(None), slice(HALO - 1, HALO + band_rows + 1), slice(HALO - 1, HALO + band_columns + 1))
    levels_float = jnp.arange(VERTICAL_STRATA).astype(jnp.float32)[:, None, None]
    wet_wide = (levels_float < depth_ext[None][near]).astype(jnp.float32)
    tracer_wide = ext[4:][near] * wet_wide
    centre = (slice(None), slice(1, -1), slice(1, -1))
    submerged_stratum_mask = wet_wide[centre]
    passive_scalar_values = tracer_wide[centre]
    tracer_e = east_of(tracer_wide)[centre]
    tracer_w = west_of(tracer_wide)[centre]
    tracer_n = north_of(tracer_wide)[centre]
    tracer_s = south_of(tracer_wide)[centre]
    wet_e = east_of(wet_wide)[centre]
    wet_w = west_of(wet_wide)[centre]
    wet_n = north_of(wet_wide)[centre]
    wet_s = south_of(wet_wide)[centre]
    mixing = (
        wet_e * (tracer_e - passive_scalar_values)
        + wet_w * (tracer_w - passive_scalar_values)
        + wet_n * (tracer_n - passive_scalar_values)
        + wet_s * (tracer_s - passive_scalar_values)
    )
    speed_east = east[None] + zonal_baroclinic_velocity
    speed_north = north[None] + meridional_baroclinic_velocity
    carried = speed_east * (tracer_e - tracer_w) + speed_north * (tracer_n - tracer_s)
    tracer_new = submerged_stratum_mask * (
        passive_scalar_values + mix_coef * mixing - carry_coef * carried
    )
    surface_grid = jnp.stack([height, speed_east[0], speed_north[0], tracer_new[0]])
    slots = sent_sender_mesh_index.shape[2]
    width = slots // CHUNKS
    atmosphere = 0.0
    for chunk in range(CHUNKS):
        part = slice(chunk * width, (chunk + 1) * width)
        values = pick_cells(
            surface_grid,
            sent_sender_mesh_index[0][:, part],
            sent_intersection_extent[0][:, part],
            sent_entry_tally[0] - chunk * width,
        )
        block = lax.all_to_all(values, ("lat", "lon"), split_axis=0, concat_axis=0, tiled=True)
        atmosphere = atmosphere + spread_cells(block, received_atmosphere_mesh_index[0][:, part], ACELL)
    return (height, east, north, tracer_new, atmosphere)


def solution(mesh):
    in_specs = (
        P("lat", "lon"),
        P("lat", "lon"),
        P("lat", "lon"),
        P("lat", "lon"),
        P(None, "lat", "lon"),
        P(None, "lat", "lon"),
        P(None, "lat", "lon"),
        P(("lat", "lon"), None, None),
        P(("lat", "lon"), None, None),
        P(("lat", "lon"), None),
        P(("lat", "lon"), None, None),
    )
    out_specs = (
        P("lat", "lon"),
        P("lat", "lon"),
        P("lat", "lon"),
        P(None, "lat", "lon"),
        P(None, ("lat", "lon")),
    )
    return jax.shard_map(local, mesh=mesh, in_specs=in_specs, out_specs=out_specs, check_vma=False)
```

profile of v0, /device:TPU:1, one launch (start us, length us, event | category | flops | bytes accessed | tf_op | source)
XLA Modules:
  0.0 117.8 jit_solution(11160609730888318955)
XLA Ops:
  0.6 0.7 bitcast_dynamic-update-slice_fusion.3
  1.4 0.7 copy-done.12
  2.1 0.7 copy-done.13
  2.8 1.0 constant_dynamic-update-slice_fusion
  3.8 0.1 fusion.68
  3.9 1.5 %collective-permute-start.1 = (f32[12,32,8]{2,1,0:T(8,128)S(1)}, f32[12,32,8]{2,1,0:T(8,128)S(1)}, u32[]{:S(2)}, u32[]{:S(2)}) collective-permute-start(f32[12,32,8]{2,1,0:T(8,128)S(1)} %get-tuple-element.29), channel_id=1, source_target_pairs={{1,0},{2,1},{3,2},{4,3},{5,4},{6,5},{7,6},{8,7},{9,8},{10,9},{11,1... | collective-permute-start | bytes 36872 | tf_op jit(solution)/shard_map/ppermute | solution.py:32
  5.4 3.0 %collective-permute-start = (f32[12,32,8]{2,1,0:T(8,128)S(1)}, f32[12,32,8]{2,1,0:T(8,128)S(1)}, u32[]{:S(2)}, u32[]{:S(2)}) collective-permute-start(f32[12,32,8]{2,1,0:T(8,128)S(1)} %get-tuple-element.28), channel_id=1, source_target_pairs={{0,1},{1,2},{2,3},{3,4},{4,5},{5,6},{6,7},{7,8},{8,9},{9,10},{10,1... | collective-permute-start | bytes 36872 | tf_op jit(solution)/shard_map/ppermute | solution.py:31
  8.4 0.9 fusion.67
  9.2 0.4 copy-done.4
  9.6 0.8 fusion.66
  10.4 1.2 %collective-permute-done.1 = f32[12,32,8]{2,1,0:T(8,128)S(1)} collective-permute-done((f32[12,32,8]{2,1,0:T(8,128)S(1)}, f32[12,32,8]{2,1,0:T(8,128)S(1)}, u32[]{:S(2)}, u32[]{:S(2)}) %collective-permute-start.1) | collective-permute-done | bytes 12320 | tf_op jit(solution)/shard_map/ppermute | solution.py:32
  11.6 1.4 %collective-permute-done = f32[12,32,8]{2,1,0:T(8,128)S(1)} collective-permute-done((f32[12,32,8]{2,1,0:T(8,128)S(1)}, f32[12,32,8]{2,1,0:T(8,128)S(1)}, u32[]{:S(2)}, u32[]{:S(2)}) %collective-permute-start) | collective-permute-done | bytes 12320 | tf_op jit(solution)/shard_map/ppermute | solution.py:31
  13.1 0.1 pad_maximum_fusion.6
  13.2 1.3 %collective-permute-start.4 = (f32[12,8,144]{2,1,0:T(8,128)S(1)}, f32[12,8,144]{2,1,0:T(8,128)S(1)}, u32[]{:S(2)}, u32[]{:S(2)}) collective-permute-start(f32[12,8,144]{2,1,0:T(8,128)S(1)} %get-tuple-element.21), channel_id=1, source_target_pairs={{16,0},{32,16},{48,32},{64,48},{80,64},{96,80},{112,96},{17,1},{33... | collective-permute-start | bytes 165896 | tf_op jit(solution)/shard_map/ppermute | solution.py:38
  14.5 0.7 collective-permute-start.3
  15.3 0.7 copy-done.14
  16.0 0.7 copy.23.tally_ref
  16.7 4.2 %collective-permute-start.2 = (f32[12,8,144]{2,1,0:T(8,128)S(1)}, f32[12,8,144]{2,1,0:T(8,128)S(1)}, u32[]{:S(2)}, u32[]{:S(2)}) collective-permute-start(f32[12,8,144]{2,1,0:T(8,128)S(1)} %get-tuple-element.20), channel_id=1, source_target_pairs={{0,16},{16,32},{32,48},{48,64},{64,80},{80,96},{96,112},{1,17},{17... | collective-permute-start | bytes 165896 | tf_op jit(solution)/shard_map/ppermute | solution.py:37
  20.9 0.2 reverse
  21.1 0.5 copy-done.15
  21.5 0.1 multiply_select_fusion
  21.7 0.8 collective-permute-done.2
  22.5 0.1 multiply_bitcast_fusion
  22.6 0.1 fusion.7
  22.7 0.1 fusion.8
  22.8 0.1 fusion.100
  22.9 0.1 fusion.11
  23.1 0.1 fusion.93
  23.2 0.1 fusion.25
  23.4 0.1 fusion.92
  23.5 0.1 fusion.21
  23.7 0.1 fusion.85
  23.8 0.1 fusion.37
  24.0 0.1 fusion.84
  24.1 0.1 fusion.33
  24.2 0.1 fusion.77
  24.4 0.1 fusion.49
  24.7 0.1 fusion.45
  24.9 0.1 fusion.70
  25.0 0.1 maximum_bitcast_fusion.3
  25.1 0.1 compare_convert_fusion
  25.2 0.1 fusion.53
  25.3 0.1 fusion.55
  25.5 0.3 compare_select_fusion
  25.8 0.3 copy-done.9
  26.1 0.3 copy-done.7
  26.4 0.3 fusion.4
  26.8 0.6 pad_maximum_fusion.7
  27.5 13.3 %shard_map.155 = f32[128,4,512]{2,1,0:T(4,128)} custom-call(f32[128,128]{1,0:T(8,128)} %bitcast.64, s32[128,512]{1,0:T(8,128)} %get-tuple-element.27.index_ref, f32[128,512]{1,0:T(8,128)} %get-tuple-element.25.extent_ref, s32[128,1]{1,0:T(8,128)} %copy.23.tally_ref), custom_call_target="tpu_custom_call" | custom-call | tf_op jit(solution)/shard_map/pallas_call | solution.py:108
  40.8 17.3 %all-to-all-start = ((f32[128,4,512]{2,1,0:T(4,128)}), f32[128,4,512]{2,1,0:T(4,128)S(1)}, u32[]{:S(2)}, u32[]{:S(2)}) async-start(f32[128,4,512]{2,1,0:T(4,128)} %shard_map.155), calls=%async_computation | async-start | bytes 2097152 | tf_op jit(solution)/shard_map/all_to_all | solution.py:258
  58.1 0.6 broadcast_add_fusion.2.tally_ref
  58.7 13.3 %shard_map.157 = f32[128,4,512]{2,1,0:T(4,128)} custom-call(f32[128,128]{1,0:T(8,128)} %bitcast.65, s32[128,512]{1,0:T(8,128)} %get-tuple-element.26.index_ref, f32[128,512]{1,0:T(8,128)} %get-tuple-element.24.extent_ref, s32[128,1]{1,0:T(8,128)} %broadcast_add_fusion.2.tally_ref), custom_call_target="tpu_custom_call" | custom-call | tf_op jit(solution)/shard_map/pallas_call | solution.py:108
  72.0 5.1 %all-to-all-done.value_ref = f32[128,4,512]{2,1,0:T(4,128)S(1)} async-done(((f32[128,4,512]{2,1,0:T(4,128)}), f32[128,4,512]{2,1,0:T(4,128)S(1)}, u32[]{:S(2)}, u32[]{:S(2)}) %all-to-all-start) | async-done | bytes 1048608 | tf_op jit(solution)/shard_map/all_to_all | solution.py:258
  77.1 1.0 copy-done
  78.1 4.7 %all-to-all-start.1 = ((f32[128,4,512]{2,1,0:T(4,128)}), f32[128,4,512]{2,1,0:T(4,128)S(1)}, u32[]{:S(2)}, u32[]{:S(2)}) async-start(f32[128,4,512]{2,1,0:T(4,128)} %shard_map.157), calls=%async_computation.1 | async-start | bytes 2097152 | tf_op jit(solution)/shard_map/all_to_all | solution.py:258
  82.8 0.8 fusion.65
  83.6 0.7 slice.461
  84.3 13.3 %shard_map.156 = f32[128,256]{1,0:T(8,128)} custom-call(f32[128,4,512]{2,1,0:T(4,128)} %copy-done, s32[128,512]{1,0:T(8,128)} %get-tuple-element.23.target_ref), custom_call_target="tpu_custom_call" | custom-call | tf_op jit(solution)/shard_map/pallas_call | solution.py:161
  97.6 1.0 copy.24
  98.6 3.2 %all-to-all-done.1.value_ref = f32[128,4,512]{2,1,0:T(4,128)S(1)} async-done(((f32[128,4,512]{2,1,0:T(4,128)}), f32[128,4,512]{2,1,0:T(4,128)S(1)}, u32[]{:S(2)}, u32[]{:S(2)}) %all-to-all-start.1) | async-done | bytes 1048608 | tf_op jit(solution)/shard_map/all_to_all | solution.py:258
  101.8 1.0 copy-done.1
  102.8 13.3 %shard_map.158 = f32[128,256]{1,0:T(8,128)} custom-call(f32[128,4,512]{2,1,0:T(4,128)} %copy-done.1, s32[128,512]{1,0:T(8,128)} %get-tuple-element.22.target_ref), custom_call_target="tpu_custom_call" | custom-call | tf_op jit(solution)/shard_map/pallas_call | solution.py:161
  116.1 1.0 copy.27
  117.2 0.7 copy.30
  (63 shorter events, 1.2 us)
Async XLA Ops:
  0.6 0.7 copy-start.11
  1.4 0.7 copy-start.12
  2.1 0.7 copy-start.13
  2.8 5.5 %copy-start.3 = (s32[1,128,1024]{2,1,0:T(8,128)S(1)}, s32[1,128,1024]{2,1,0:T(8,128)}, u32[]{:S(2)}) copy-start(s32[1,128,1024]{2,1,0:T(8,128)} %param.19) | copy-start | bytes 1572868
  3.9 7.7 %collective-permute-start.1 = (f32[12,32,8]{2,1,0:T(8,128)S(1)}, f32[12,32,8]{2,1,0:T(8,128)S(1)}, u32[]{:S(2)}, u32[]{:S(2)}) collective-permute-start(f32[12,32,8]{2,1,0:T(8,128)S(1)} %get-tuple-element.29), channel_id=1, source_target_pairs={{1,0},{2,1},{3,2},{4,3},{5,4},{6,5},{7,6},{8,7},{9,8},{10,9},{11,1... | collective-permute-start | bytes 36872 | tf_op jit(solution)/shard_map/ppermute | solution.py:32
  5.4 7.7 %collective-permute-start = (f32[12,32,8]{2,1,0:T(8,128)S(1)}, f32[12,32,8]{2,1,0:T(8,128)S(1)}, u32[]{:S(2)}, u32[]{:S(2)}) collective-permute-start(f32[12,32,8]{2,1,0:T(8,128)S(1)} %get-tuple-element.28), channel_id=1, source_target_pairs={{0,1},{1,2},{2,3},{3,4},{4,5},{5,6},{6,7},{7,8},{8,9},{9,10},{10,1... | collective-permute-start | bytes 36872 | tf_op jit(solution)/shard_map/ppermute | solution.py:31
  8.4 1.2 %copy-start.4 = (f32[1,128,1024]{2,1,0:T(8,128)S(1)}, f32[1,128,1024]{2,1,0:T(8,128)}, u32[]{:S(2)}) copy-start(f32[1,128,1024]{2,1,0:T(8,128)} %param.20) | copy-start | bytes 1572868
  13.2 7.9 %collective-permute-start.4 = (f32[12,8,144]{2,1,0:T(8,128)S(1)}, f32[12,8,144]{2,1,0:T(8,128)S(1)}, u32[]{:S(2)}, u32[]{:S(2)}) collective-permute-start(f32[12,8,144]{2,1,0:T(8,128)S(1)} %get-tuple-element.21), channel_id=1, source_target_pairs={{16,0},{32,16},{48,32},{64,48},{80,64},{96,80},{112,96},{17,1},{33... | collective-permute-start | bytes 165896 | tf_op jit(solution)/shard_map/ppermute | solution.py:38
  14.5 6.4 %collective-permute-start.3 = (f32[12,8,144]{2,1,0:T(8,128)S(1)}, f32[12,8,144]{2,1,0:T(8,128)S(1)}, u32[]{:S(2)}, u32[]{:S(2)}) collective-permute-start(f32[12,8,144]{2,1,0:T(8,128)S(1)} %get-tuple-element.20), channel_id=1, source_target_pairs={{112,127},{113,126},{114,125},{115,124},{116,123},{117,122},{118,1... | collective-permute-start | bytes 165896 | tf_op jit(solution)/shard_map/ppermute | solution.py:41
  15.3 0.7 copy-start.14
  16.7 5.8 %collective-permute-start.2 = (f32[12,8,144]{2,1,0:T(8,128)S(1)}, f32[12,8,144]{2,1,0:T(8,128)S(1)}, u32[]{:S(2)}, u32[]{:S(2)}) collective-permute-start(f32[12,8,144]{2,1,0:T(8,128)S(1)} %get-tuple-element.20), channel_id=1, source_target_pairs={{0,16},{16,32},{32,48},{48,64},{64,80},{80,96},{96,112},{1,17},{17... | collective-permute-start | bytes 165896 | tf_op jit(solution)/shard_map/ppermute | solution.py:37
  20.9 0.7 copy-start.15
  25.5 0.6 copy-start.9
  25.5 0.6 copy-start.10
  25.5 0.9 copy-start.7
  25.5 1.0 copy-start.8
  26.8 14.0 %copy-start.6 = (f32[8,32,128]{2,1,0:T(8,128)}, f32[8,32,128]{2,1,0:T(8,128)S(1)}, u32[]{:S(2)}) copy-start(f32[8,32,128]{2,1,0:T(8,128)S(1)} %get-tuple-element.5) | copy-start | bytes 393220
  40.8 17.3 %copy-start.2 = (s32[128,1]{1,0:T(8,128)S(1)}, s32[128,1]{1,0:T(8,128)}, u32[]{:S(2)}) copy-start(s32[128,1]{1,0:T(8,128)} %copy.23.tally_ref) | copy-start | bytes 1540
  40.8 36.3 %all-to-all-start = ((f32[128,4,512]{2,1,0:T(4,128)}), f32[128,4,512]{2,1,0:T(4,128)S(1)}, u32[]{:S(2)}, u32[]{:S(2)}) async-start(f32[128,4,512]{2,1,0:T(4,128)} %shard_map.155), calls=%async_computation | async-start | bytes 2097152 | tf_op jit(solution)/shard_map/all_to_all | solution.py:258
  72.0 10.8 %copy-start.5 = (s32[1,128,1024]{2,1,0:T(8,128)S(1)}, s32[1,128,1024]{2,1,0:T(8,128)}, u32[]{:S(2)}) copy-start(s32[1,128,1024]{2,1,0:T(8,128)} %param.22) | copy-start | bytes 1572868
  77.1 1.0 copy-start
  78.1 23.7 %all-to-all-start.1 = ((f32[128,4,512]{2,1,0:T(4,128)}), f32[128,4,512]{2,1,0:T(4,128)S(1)}, u32[]{:S(2)}, u32[]{:S(2)}) async-start(f32[128,4,512]{2,1,0:T(4,128)} %shard_map.157), calls=%async_computation.1 | async-start | bytes 2097152 | tf_op jit(solution)/shard_map/all_to_all | solution.py:258
  101.8 1.0 copy-start.1
where the time goes:
time: 119 us; the launch traced here: 118 us
  Pallas kernels  53.2 us (45%)
  starting transfers between devices  32.5 us (27%)
  local copies, waits for them, and re-layouts  15.7 us (13%)
  waiting for transfers between devices  11.8 us (10%)
  other arithmetic  3.58 us (3%)
    pallas_call x2, Pallas kernels, spread_cells(): pl.pallas_call(spread_kernel, out_shape=jax.ShapeDtypeStruct((lows, 2 * f...  26.6 us
    pallas_call x2, Pallas kernels, pick_cells(): pl.pallas_call(pick_kernel, out_shape=jax.ShapeDtypeStruct((owners, field...  26.6 us
    all_to_all x2, starting transfers between devices, local(): lax.all_to_all(values, ('lat', 'lon'), split_axis=0, concat_axis=0, tiled...  22 us
    all_to_all x2, waiting for transfers between devices, local(): lax.all_to_all(values, ('lat', 'lon'), split_axis=0, concat_axis=0, tiled...  8.28 us
    unnamed x37, local copies, waits for them, and re-layouts  7.22 us
    ppermute x1, starting transfers between devices, exchange(): from_south = lax.ppermute(top, 'lat', upward)  4.16 us
    ppermute x1, starting transfers between devices, exchange(): from_west = lax.ppermute(block[:, :, columns - width:], 'lon', eastward)  2.99 us
  transfers between devices with their start and end apart: 7, of which 5 were waited for; matrix products, arithmetic and copies ran while one was open for 5% of the time, Pallas kernels for 23%

commit v1 on v0

--- a/solution.py
+++ b/solution.py
@@ -1,3 +1,4 @@
+import functools
 import math
 
 import jax
@@ -71,7 +72,7 @@
     return high, low
 
 
-def pick_kernel(table_ref, index_ref, extent_ref, tally_ref, out_ref):
+def pick_kernel(offset, table_ref, index_ref, extent_ref, tally_ref, out_ref):
     fields_count = out_ref.shape[1]
     slots = index_ref.shape[1]
     table_rows = table_ref.shape[0]
@@ -80,7 +81,7 @@
     table = jnp.concatenate(split_pieces(table_ref[...]), axis=1)
     column_ids = lax.broadcasted_iota(jnp.int32, (columns, slots), 0)
     row_ids = lax.broadcasted_iota(jnp.int32, (8, slots), 0)
-    slot_ids = lax.broadcasted_iota(jnp.int32, (1, slots), 1)
+    slot_ids = lax.broadcasted_iota(jnp.int32, (1, slots), 1) + offset
     for owner in range(index_ref.shape[0]):
         index = index_ref[pl.ds(owner, 1), :]
         hot = (column_ids == index % columns).astype(jnp.bfloat16)
@@ -101,25 +102,25 @@
             out_ref[owner, pl.ds(field, 1), :] = picked * weight
 
 
-def pick_cells(surface_grid, indices, extent, tally):
+def pick_cells(surface_grid, indices, extent, tally, chunk, slots):
     fields_count, rows, columns = surface_grid.shape
-    owners, slots = indices.shape
+    owners = indices.shape[0]
     table = surface_grid.reshape(fields_count * rows, columns)
     return pl.pallas_call(
-        pick_kernel,
+        functools.partial(pick_kernel, chunk * slots),
         out_shape=jax.ShapeDtypeStruct((owners, fields_count, slots), jnp.float32),
         grid=(owners // GROUP,),
         in_specs=[
             pl.BlockSpec((fields_count * rows, columns), lambda i: (0, 0)),
-            pl.BlockSpec((GROUP, slots), lambda i: (i, 0)),
-            pl.BlockSpec((GROUP, slots), lambda i: (i, 0)),
+            pl.BlockSpec((GROUP, slots), lambda i: (i, chunk)),
+            pl.BlockSpec((GROUP, slots), lambda i: (i, chunk)),
             pl.BlockSpec((GROUP, 1), lambda i: (i, 0)),
         ],
         out_specs=pl.BlockSpec((GROUP, fields_count, slots), lambda i: (i, 0, 0)),
     )(table, indices, extent, tally[:, None])
 
 
-def spread_kernel(value_ref, target_ref, out_ref):
+def spread_kernel(value_ref, target_ref, start_ref, out_ref):
     fields_count = value_ref.shape[1]
     slots = value_ref.shape[2]
     lows = out_ref.shape[0]
@@ -127,7 +128,7 @@
 
     @pl.when(pl.program_id(0) == 0)
     def _():
-        out_ref[...] = jnp.zeros_like(out_ref)
+        out_ref[...] = start_ref[...]
 
     high_ids = lax.broadcasted_iota(jnp.int32, (highs, slots), 0)
     low_ids = lax.broadcasted_iota(jnp.int32, (lows, slots), 0)
@@ -154,22 +155,24 @@
     out_ref[...] += total
 
 
-def spread_cells(values, targets, cells):
+SPREAD_LOWS = 128
+
+
+def spread_cells(values, targets, chunk, start):
     senders, fields_count, slots = values.shape
-    lows = 128
-    highs = cells // lows
-    summed = pl.pallas_call(
+    shape = start.shape
+    return pl.pallas_call(
         spread_kernel,
-        out_shape=jax.ShapeDtypeStruct((lows, 2 * fields_count * highs), jnp.float32),
+        out_shape=jax.ShapeDtypeStruct(shape, jnp.float32),
         grid=(senders // GROUP,),
         in_specs=[
             pl.BlockSpec((GROUP, fields_count, slots), lambda i: (i, 0, 0)),
-            pl.BlockSpec((GROUP, slots), lambda i: (i, 0)),
+            pl.BlockSpec((GROUP, slots), lambda i: (i, chunk)),
+            pl.BlockSpec(shape, lambda i: (0, 0)),
         ],
-        out_specs=pl.BlockSpec((lows, 2 * fields_count * highs), lambda i: (0, 0)),
-    )(values, targets)
-    summed = summed.reshape(lows, 2, fields_count, highs).sum(axis=1)
-    return jnp.transpose(summed, (1, 2, 0)).reshape(fields_count, cells)
+        out_specs=pl.BlockSpec(shape, lambda i: (0, 0)),
+        input_output_aliases={2: 0},
+    )(values, targets, start)
 
 
 def local(
@@ -246,17 +249,21 @@
     surface_grid = jnp.stack([height, speed_east[0], speed_north[0], tracer_new[0]])
     slots = sent_sender_mesh_index.shape[2]
     width = slots // CHUNKS
-    atmosphere = 0.0
+    highs = ACELL // SPREAD_LOWS
+    summed = jnp.zeros((SPREAD_LOWS, 2 * NF * highs), jnp.float32)
     for chunk in range(CHUNKS):
-        part = slice(chunk * width, (chunk + 1) * width)
         values = pick_cells(
             surface_grid,
-            sent_sender_mesh_index[0][:, part],
-            sent_intersection_extent[0][:, part],
-            sent_entry_tally[0] - chunk * width,
+            sent_sender_mesh_index[0],
+            sent_intersection_extent[0],
+            sent_entry_tally[0],
+            chunk,
+            width,
         )
         block = lax.all_to_all(values, ("lat", "lon"), split_axis=0, concat_axis=0, tiled=True)
-        atmosphere = atmosphere + spread_cells(block, received_atmosphere_mesh_index[0][:, part], ACELL)
+        summed = spread_cells(block, received_atmosphere_mesh_index[0], chunk, summed)
+    summed = summed.reshape(SPREAD_LOWS, 2, NF, highs).sum(axis=1)
+    atmosphere = jnp.transpose(summed, (1, 2, 0)).reshape(NF, ACELL)
     return (height, east, north, tracer_new, atmosphere)
 
 

time: 119 us -> 116 us (0.975)
  waiting for transfers between devices: 11.8 us -> 18 us
  starting transfers between devices: 32.5 us -> 27.6 us
  local copies, waits for them, and re-layouts: 15.7 us -> 12.4 us
    all_to_all x2, starting transfers between devices: 22 us -> 17 us  [local(): lax.all_to_all(values, ('lat', 'lon'), split_axis=0, concat_axis=0, tiled...]
    ppermute x1, waiting for transfers between devices: 1.19 us -> 4.6 us  [exchange(): from_east = lax.ppermute(block[:, :, :width], 'lon', westward)]
    slice x3 -> x0, local copies, waits for them, and re-layouts: 2.53 us -> none  [the longest x1 0.85 us: local(): sent_sender_mesh_index[0][:, part]]
    all_to_all x2, waiting for transfers between devices: 8.28 us -> 9.84 us  [local(): lax.all_to_all(values, ('lat', 'lon'), split_axis=0, concat_axis=0, tiled...]
    ppermute x1, starting transfers between devices: 1.45 us -> 0.01 us  [exchange(): from_east = lax.ppermute(block[:, :, :width], 'lon', westward)]
    ppermute x1, starting transfers between devices: 2.99 us -> 4.36 us  [exchange(): from_west = lax.ppermute(block[:, :, columns - width:], 'lon', eastward)]
    unnamed x37 -> x29, local copies, waits for them, and re-layouts: 7.22 us -> 6.83 us
  transfers between devices with their start and end apart: 7 -> 7, of which waited for: 5 -> 5; matrix products, arithmetic and copies ran while one was open for 5% -> 2% of each run, Pallas kernels for 23% -> 23%
where the time goes in v1:
time: 116 us; the launch traced here: 115 us
  Pallas kernels  53.5 us (46%)
  starting transfers between devices  27.6 us (24%)
  waiting for transfers between devices  18 us (16%)
  local copies, waits for them, and re-layouts  12.4 us (11%)
  other arithmetic  2.94 us (3%)
    pallas_call x2, Pallas kernels, spread_cells(): pl.pallas_call(spread_kernel, out_shape=jax.ShapeDtypeStruct(shape, jnp.f...  26.9 us
    pallas_call x2, Pallas kernels, pick_cells(): pl.pallas_call(functools.partial(pick_kernel, chunk * slots), out_shape=j...  26.6 us
    all_to_all x2, starting transfers between devices, local(): lax.all_to_all(values, ('lat', 'lon'), split_axis=0, concat_axis=0, tiled...  17 us
    all_to_all x2, waiting for transfers between devices, local(): lax.all_to_all(values, ('lat', 'lon'), split_axis=0, concat_axis=0, tiled...  9.84 us
    unnamed x29, local copies, waits for them, and re-layouts  6.83 us
    ppermute x1, waiting for transfers between devices, exchange(): from_east = lax.ppermute(block[:, :, :width], 'lon', westward)  4.6 us
    ppermute x1, starting transfers between devices, exchange(): from_west = lax.ppermute(block[:, :, columns - width:], 'lon', eastward)  4.36 us
    ppermute x1, starting transfers between devices, exchange(): from_south = lax.ppermute(top, 'lat', upward)  4.27 us
  transfers between devices with their start and end apart: 7, of which 5 were waited for; matrix products, arithmetic and copies ran while one was open for 2% of the time, Pallas kernels for 23%

profile of v1, /device:TPU:1, one launch (start us, length us, event | category | flops | bytes accessed | tf_op | source)
XLA Modules:
  0.0 115.5 jit_solution(6282846552227618193)
XLA Ops:
  0.6 0.7 bitcast_dynamic-update-slice_fusion.3
  1.4 0.7 copy-done.8
  2.1 0.7 copy-done.9
  2.8 0.9 constant_dynamic-update-slice_fusion
  3.7 0.1 fusion.65
  3.8 4.4 %collective-permute-start = (f32[12,32,8]{2,1,0:T(8,128)S(1)}, f32[12,32,8]{2,1,0:T(8,128)S(1)}, u32[]{:S(2)}, u32[]{:S(2)}) collective-permute-start(f32[12,32,8]{2,1,0:T(8,128)S(1)} %get-tuple-element.22), channel_id=1, source_target_pairs={{0,1},{1,2},{2,3},{3,4},{4,5},{5,6},{6,7},{7,8},{8,9},{9,10},{10,1... | collective-permute-start | bytes 36872 | tf_op jit(solution)/shard_map/ppermute | solution.py:32
  8.2 2.6 %collective-permute-done = f32[12,32,8]{2,1,0:T(8,128)S(1)} collective-permute-done((f32[12,32,8]{2,1,0:T(8,128)S(1)}, f32[12,32,8]{2,1,0:T(8,128)S(1)}, u32[]{:S(2)}, u32[]{:S(2)}) %collective-permute-start) | collective-permute-done | bytes 12320 | tf_op jit(solution)/shard_map/ppermute | solution.py:32
  10.8 4.6 %collective-permute-done.1 = f32[12,32,8]{2,1,0:T(8,128)S(1)} collective-permute-done((f32[12,32,8]{2,1,0:T(8,128)S(1)}, f32[12,32,8]{2,1,0:T(8,128)S(1)}, u32[]{:S(2)}, u32[]{:S(2)}) %collective-permute-start.1) | collective-permute-done | bytes 12320 | tf_op jit(solution)/shard_map/ppermute | solution.py:33
  15.4 0.1 pad_maximum_fusion.6
  15.6 0.7 collective-permute-start.3
  16.2 1.3 %collective-permute-start.4 = (f32[12,8,144]{2,1,0:T(8,128)S(1)}, f32[12,8,144]{2,1,0:T(8,128)S(1)}, u32[]{:S(2)}, u32[]{:S(2)}) collective-permute-start(f32[12,8,144]{2,1,0:T(8,128)S(1)} %get-tuple-element.21), channel_id=1, source_target_pairs={{16,0},{32,16},{48,32},{64,48},{80,64},{96,80},{112,96},{17,1},{33... | collective-permute-start | bytes 165896 | tf_op jit(solution)/shard_map/ppermute | solution.py:39
  17.7 0.7 copy-done.10
  18.3 0.7 copy.21.tally_ref
  19.1 4.3 %collective-permute-start.2 = (f32[12,8,144]{2,1,0:T(8,128)S(1)}, f32[12,8,144]{2,1,0:T(8,128)S(1)}, u32[]{:S(2)}, u32[]{:S(2)}) collective-permute-start(f32[12,8,144]{2,1,0:T(8,128)S(1)} %get-tuple-element.20), channel_id=1, source_target_pairs={{0,16},{16,32},{32,48},{48,64},{64,80},{80,96},{96,112},{1,17},{17... | collective-permute-start | bytes 165896 | tf_op jit(solution)/shard_map/ppermute | solution.py:38
  23.4 0.2 reverse
  23.5 0.5 copy-done.11
  24.0 0.1 multiply_select_fusion
  24.1 0.9 collective-permute-done.2
  25.1 0.1 multiply_bitcast_fusion
  25.1 0.1 fusion.7
  25.2 0.1 fusion.8
  25.3 0.1 fusion.97
  25.4 0.1 fusion.96
  25.5 0.1 fusion.11
  25.6 0.1 fusion.90
  25.7 0.1 fusion.91
  25.8 0.1 fusion.25
  25.9 0.1 fusion.89
  26.0 0.1 fusion.88
  26.1 0.1 fusion.21
  26.2 0.1 fusion.82
  26.3 0.1 fusion.83
  26.4 0.1 fusion.37
  26.5 0.1 fusion.81
  26.6 0.1 fusion.33
  26.7 0.1 fusion.74
  26.8 0.1 fusion.75
  26.9 0.1 fusion.49
  27.0 0.1 fusion.73
  27.2 0.1 fusion.45
  27.3 0.1 fusion.67
  27.6 0.1 maximum_bitcast_fusion.3
  27.7 0.1 compare_convert_fusion
  27.8 0.1 fusion.53
  27.9 0.1 fusion.55
  28.0 0.3 compare_select_fusion
  28.3 0.3 copy-done.5
  28.6 0.3 copy-done.3
  29.0 0.3 fusion.4
  29.4 0.7 pad_maximum_fusion.7
  30.0 13.3 %shard_map.156 = f32[128,4,512]{2,1,0:T(4,128)} custom-call(f32[128,128]{1,0:T(8,128)} %bitcast.68, s32[128,1024]{1,0:T(8,128)} %bitcast.62, f32[128,1024]{1,0:T(8,128)} %bitcast.64, s32[128,1]{1,0:T(8,128)} %copy.21.tally_ref), custom_call_target="tpu_custom_call" | custom-call | tf_op jit(solution)/shard_map/pallas_call | solution.py:109
  43.3 12.7 %all-to-all-start.1 = ((f32[128,4,512]{2,1,0:T(4,128)}), f32[128,4,512]{2,1,0:T(4,128)S(1)}, u32[]{:S(2)}, u32[]{:S(2)}) async-start(f32[128,4,512]{2,1,0:T(4,128)} %shard_map.156), calls=%async_computation.1 | async-start | bytes 2097152 | tf_op jit(solution)/shard_map/all_to_all | solution.py:263
  56.0 13.4 %shard_map.155 = f32[128,4,512]{2,1,0:T(4,128)} custom-call(f32[128,128]{1,0:T(8,128)} %bitcast.69, s32[128,1024]{1,0:T(8,128)} %bitcast.63, f32[128,1024]{1,0:T(8,128)} %bitcast.65, s32[128,1]{1,0:T(8,128)} %copy.21.tally_ref), custom_call_target="tpu_custom_call" | custom-call | tf_op jit(solution)/shard_map/pallas_call | solution.py:109
  69.4 5.6 %all-to-all-done.1.value_ref = f32[128,4,512]{2,1,0:T(4,128)S(1)} async-done(((f32[128,4,512]{2,1,0:T(4,128)}), f32[128,4,512]{2,1,0:T(4,128)S(1)}, u32[]{:S(2)}, u32[]{:S(2)}) %all-to-all-start.1) | async-done | bytes 1048608 | tf_op jit(solution)/shard_map/all_to_all | solution.py:263
  75.0 1.0 copy-done
  76.0 4.3 %all-to-all-start = ((f32[128,4,512]{2,1,0:T(4,128)}), f32[128,4,512]{2,1,0:T(4,128)S(1)}, u32[]{:S(2)}, u32[]{:S(2)}) async-start(f32[128,4,512]{2,1,0:T(4,128)} %shard_map.155), calls=%async_computation | async-start | bytes 2097152 | tf_op jit(solution)/shard_map/all_to_all | solution.py:263
  80.3 0.7 slice.437
  81.0 0.7 broadcast_in_dim.2.start_ref
  81.7 13.5 %shard_map.157.start_ref = f32[128,256]{1,0:T(8,128)} custom-call(f32[128,4,512]{2,1,0:T(4,128)} %copy-done, s32[128,1024]{1,0:T(8,128)} %bitcast.66, f32[128,256]{1,0:T(8,128)} %broadcast_in_dim.2.start_ref), custom_call_target="tpu_custom_call", output_to_operand_aliasing={{}: (2, {})} | custom-call | tf_op jit(solution)/shard_map/pallas_call | solution.py:164
  95.2 4.2 %all-to-all-done.value_ref = f32[128,4,512]{2,1,0:T(4,128)S(1)} async-done(((f32[128,4,512]{2,1,0:T(4,128)}), f32[128,4,512]{2,1,0:T(4,128)S(1)}, u32[]{:S(2)}, u32[]{:S(2)}) %all-to-all-start) | async-done | bytes 1048608 | tf_op jit(solution)/shard_map/all_to_all | solution.py:263
  99.3 1.0 copy-done.1
  100.4 13.4 %shard_map.158 = f32[128,256]{1,0:T(8,128)} custom-call(f32[128,4,512]{2,1,0:T(4,128)} %copy-done.1, s32[128,1024]{1,0:T(8,128)} %bitcast.67, f32[128,256]{1,0:T(8,128)} %shard_map.157.start_ref), custom_call_target="tpu_custom_call", output_to_operand_aliasing={{}: (2, {})} | custom-call | tf_op jit(solution)/shard_map/pallas_call | solution.py:164
  113.8 1.0 copy.23
  114.8 0.7 copy.26
  (49 shorter events, 0.7 us)
Async XLA Ops:
  0.6 0.7 copy-start.7
  1.4 0.7 copy-start.8
  2.1 0.7 copy-start.9
  3.8 7.0 %collective-permute-start = (f32[12,32,8]{2,1,0:T(8,128)S(1)}, f32[12,32,8]{2,1,0:T(8,128)S(1)}, u32[]{:S(2)}, u32[]{:S(2)}) collective-permute-start(f32[12,32,8]{2,1,0:T(8,128)S(1)} %get-tuple-element.22), channel_id=1, source_target_pairs={{0,1},{1,2},{2,3},{3,4},{4,5},{5,6},{6,7},{7,8},{8,9},{9,10},{10,1... | collective-permute-start | bytes 36872 | tf_op jit(solution)/shard_map/ppermute | solution.py:32
  8.2 7.2 %collective-permute-start.1 = (f32[12,32,8]{2,1,0:T(8,128)S(1)}, f32[12,32,8]{2,1,0:T(8,128)S(1)}, u32[]{:S(2)}, u32[]{:S(2)}) collective-permute-start(f32[12,32,8]{2,1,0:T(8,128)S(1)} %get-tuple-element.23), channel_id=1, source_target_pairs={{1,0},{2,1},{3,2},{4,3},{5,4},{6,5},{7,6},{8,7},{9,8},{10,9},{11,1... | collective-permute-start | bytes 36872 | tf_op jit(solution)/shard_map/ppermute | solution.py:33
  15.6 7.8 %collective-permute-start.3 = (f32[12,8,144]{2,1,0:T(8,128)S(1)}, f32[12,8,144]{2,1,0:T(8,128)S(1)}, u32[]{:S(2)}, u32[]{:S(2)}) collective-permute-start(f32[12,8,144]{2,1,0:T(8,128)S(1)} %get-tuple-element.20), channel_id=1, source_target_pairs={{112,127},{113,126},{114,125},{115,124},{116,123},{117,122},{118,1... | collective-permute-start | bytes 165896 | tf_op jit(solution)/shard_map/ppermute | solution.py:42
  16.2 7.3 %collective-permute-start.4 = (f32[12,8,144]{2,1,0:T(8,128)S(1)}, f32[12,8,144]{2,1,0:T(8,128)S(1)}, u32[]{:S(2)}, u32[]{:S(2)}) collective-permute-start(f32[12,8,144]{2,1,0:T(8,128)S(1)} %get-tuple-element.21), channel_id=1, source_target_pairs={{16,0},{32,16},{48,32},{64,48},{80,64},{96,80},{112,96},{17,1},{33... | collective-permute-start | bytes 165896 | tf_op jit(solution)/shard_map/ppermute | solution.py:39
  17.7 0.7 copy-start.10
  19.1 6.0 %collective-permute-start.2 = (f32[12,8,144]{2,1,0:T(8,128)S(1)}, f32[12,8,144]{2,1,0:T(8,128)S(1)}, u32[]{:S(2)}, u32[]{:S(2)}) collective-permute-start(f32[12,8,144]{2,1,0:T(8,128)S(1)} %get-tuple-element.20), channel_id=1, source_target_pairs={{0,16},{16,32},{32,48},{48,64},{64,80},{80,96},{96,112},{1,17},{17... | collective-permute-start | bytes 165896 | tf_op jit(solution)/shard_map/ppermute | solution.py:38
  23.4 0.7 copy-start.11
  28.0 0.6 copy-start.5
  28.0 0.6 copy-start.6
  28.0 0.9 copy-start.3
  28.0 1.0 copy-start.4
  29.3 14.0 %copy-start.2 = (f32[8,32,128]{2,1,0:T(8,128)}, f32[8,32,128]{2,1,0:T(8,128)S(1)}, u32[]{:S(2)}) copy-start(f32[8,32,128]{2,1,0:T(8,128)S(1)} %get-tuple-element.5) | copy-start | bytes 393220
  43.3 31.7 %all-to-all-start.1 = ((f32[128,4,512]{2,1,0:T(4,128)}), f32[128,4,512]{2,1,0:T(4,128)S(1)}, u32[]{:S(2)}, u32[]{:S(2)}) async-start(f32[128,4,512]{2,1,0:T(4,128)} %shard_map.156), calls=%async_computation.1 | async-start | bytes 2097152 | tf_op jit(solution)/shard_map/all_to_all | solution.py:263
  75.0 1.0 copy-start
  76.0 23.3 %all-to-all-start = ((f32[128,4,512]{2,1,0:T(4,128)}), f32[128,4,512]{2,1,0:T(4,128)S(1)}, u32[]{:S(2)}, u32[]{:S(2)}) async-start(f32[128,4,512]{2,1,0:T(4,128)} %shard_map.155), calls=%async_computation | async-start | bytes 2097152 | tf_op jit(solution)/shard_map/all_to_all | solution.py:263
  99.3 1.0 copy-start.1

commit v2 on v1

--- a/solution.py
+++ b/solution.py
@@ -123,8 +123,8 @@
 def spread_kernel(value_ref, target_ref, start_ref, out_ref):
     fields_count = value_ref.shape[1]
     slots = value_ref.shape[2]
-    lows = out_ref.shape[0]
-    highs = out_ref.shape[1] // (2 * fields_count)
+    lows = out_ref.shape[1]
+    highs = out_ref.shape[0] // (2 * fields_count)
 
     @pl.when(pl.program_id(0) == 0)
     def _():
@@ -150,7 +150,7 @@
             axis=0,
         )
         total = total + lax.dot_general(
-            low_hot, weighted, (((1,), (1,)), ((), ())), preferred_element_type=jnp.float32
+            weighted, low_hot, (((1,), (1,)), ((), ())), preferred_element_type=jnp.float32
         )
     out_ref[...] += total
 
@@ -250,7 +250,7 @@
     slots = sent_sender_mesh_index.shape[2]
     width = slots // CHUNKS
     highs = ACELL // SPREAD_LOWS
-    summed = jnp.zeros((SPREAD_LOWS, 2 * NF * highs), jnp.float32)
+    summed = jnp.zeros((2 * NF * highs, SPREAD_LOWS), jnp.float32)
     for chunk in range(CHUNKS):
         values = pick_cells(
             surface_grid,
@@ -262,8 +262,7 @@
         )
         block = lax.all_to_all(values, ("lat", "lon"), split_axis=0, concat_axis=0, tiled=True)
         summed = spread_cells(block, received_atmosphere_mesh_index[0], chunk, summed)
-    summed = summed.reshape(SPREAD_LOWS, 2, NF, highs).sum(axis=1)
-    atmosphere = jnp.transpose(summed, (1, 2, 0)).reshape(NF, ACELL)
+    atmosphere = summed.reshape(2, NF, ACELL).sum(axis=0)
     return (height, east, north, tracer_new, atmosphere)
 
 

time: 116 us -> 114 us (0.983)
  Pallas kernels: 53.5 us -> 49.3 us
  waiting for transfers between devices: 18 us -> 20.2 us
    pallas_call x2, Pallas kernels: 26.9 us -> 22.6 us  [spread_cells(): pl.pallas_call(spread_kernel, out_shape=jax.ShapeDtypeStruct(shape, jnp.f...]
    all_to_all x2, waiting for transfers between devices: 9.84 us -> 12 us  [local(): lax.all_to_all(values, ('lat', 'lon'), split_axis=0, concat_axis=0, tiled...]
    unnamed x29 -> x28, local copies, waits for them, and re-layouts: 6.83 us -> 6.15 us
  transfers between devices with their start and end apart: 7 -> 7, of which waited for: 5 -> 5; matrix products, arithmetic and copies ran while one was open for 2% -> 2% of each run, Pallas kernels for 23% -> 22%
where the time goes in v2:
time: 114 us; the launch traced here: 113 us
  Pallas kernels  49.3 us (43%)
  starting transfers between devices  27.6 us (24%)
  waiting for transfers between devices  20.2 us (18%)
  local copies, waits for them, and re-layouts  11.7 us (10%)
  other arithmetic  3.59 us (3%)
    pallas_call x2, Pallas kernels, pick_cells(): pl.pallas_call(functools.partial(pick_kernel, chunk * slots), out_shape=j...  26.6 us
    pallas_call x2, Pallas kernels, spread_cells(): pl.pallas_call(spread_kernel, out_shape=jax.ShapeDtypeStruct(shape, jnp.f...  22.6 us
    all_to_all x2, starting transfers between devices, local(): lax.all_to_all(values, ('lat', 'lon'), split_axis=0, concat_axis=0, tiled...  17 us
    all_to_all x2, waiting for transfers between devices, local(): lax.all_to_all(values, ('lat', 'lon'), split_axis=0, concat_axis=0, tiled...  12 us
    unnamed x28, local copies, waits for them, and re-layouts  6.15 us
    ppermute x1, waiting for transfers between devices, exchange(): from_east = lax.ppermute(block[:, :, :width], 'lon', westward)  4.6 us
    ppermute x1, starting transfers between devices, exchange(): from_west = lax.ppermute(block[:, :, columns - width:], 'lon', eastward)  4.36 us
    ppermute x1, starting transfers between devices, exchange(): from_south = lax.ppermute(top, 'lat', upward)  4.27 us
  transfers between devices with their start and end apart: 7, of which 5 were waited for; matrix products, arithmetic and copies ran while one was open for 2% of the time, Pallas kernels for 22%

profile of v2, /device:TPU:1, one launch (start us, length us, event | category | flops | bytes accessed | tf_op | source)
XLA Modules:
  0.0 113.3 jit_solution(2690283920951758150)
XLA Ops:
  0.6 0.7 bitcast_dynamic-update-slice_fusion.3
  1.4 0.7 copy-done.8
  2.1 0.7 copy-done.9
  2.8 0.9 constant_dynamic-update-slice_fusion
  3.7 0.1 fusion.65
  3.8 4.4 %collective-permute-start = (f32[12,32,8]{2,1,0:T(8,128)S(1)}, f32[12,32,8]{2,1,0:T(8,128)S(1)}, u32[]{:S(2)}, u32[]{:S(2)}) collective-permute-start(f32[12,32,8]{2,1,0:T(8,128)S(1)} %get-tuple-element.22), channel_id=1, source_target_pairs={{0,1},{1,2},{2,3},{3,4},{4,5},{5,6},{6,7},{7,8},{8,9},{9,10},{10,1... | collective-permute-start | bytes 36872 | tf_op jit(solution)/shard_map/ppermute | solution.py:32
  8.2 2.6 %collective-permute-done = f32[12,32,8]{2,1,0:T(8,128)S(1)} collective-permute-done((f32[12,32,8]{2,1,0:T(8,128)S(1)}, f32[12,32,8]{2,1,0:T(8,128)S(1)}, u32[]{:S(2)}, u32[]{:S(2)}) %collective-permute-start) | collective-permute-done | bytes 12320 | tf_op jit(solution)/shard_map/ppermute | solution.py:32
  10.8 4.6 %collective-permute-done.1 = f32[12,32,8]{2,1,0:T(8,128)S(1)} collective-permute-done((f32[12,32,8]{2,1,0:T(8,128)S(1)}, f32[12,32,8]{2,1,0:T(8,128)S(1)}, u32[]{:S(2)}, u32[]{:S(2)}) %collective-permute-start.1) | collective-permute-done | bytes 12320 | tf_op jit(solution)/shard_map/ppermute | solution.py:33
  15.4 0.1 pad_maximum_fusion.6
  15.6 0.7 collective-permute-start.3
  16.2 1.3 %collective-permute-start.4 = (f32[12,8,144]{2,1,0:T(8,128)S(1)}, f32[12,8,144]{2,1,0:T(8,128)S(1)}, u32[]{:S(2)}, u32[]{:S(2)}) collective-permute-start(f32[12,8,144]{2,1,0:T(8,128)S(1)} %get-tuple-element.21), channel_id=1, source_target_pairs={{16,0},{32,16},{48,32},{64,48},{80,64},{96,80},{112,96},{17,1},{33... | collective-permute-start | bytes 165896 | tf_op jit(solution)/shard_map/ppermute | solution.py:39
  17.7 0.7 copy-done.10
  18.3 0.7 copy.19.tally_ref
  19.1 4.3 %collective-permute-start.2 = (f32[12,8,144]{2,1,0:T(8,128)S(1)}, f32[12,8,144]{2,1,0:T(8,128)S(1)}, u32[]{:S(2)}, u32[]{:S(2)}) collective-permute-start(f32[12,8,144]{2,1,0:T(8,128)S(1)} %get-tuple-element.20), channel_id=1, source_target_pairs={{0,16},{16,32},{32,48},{48,64},{64,80},{80,96},{96,112},{1,17},{17... | collective-permute-start | bytes 165896 | tf_op jit(solution)/shard_map/ppermute | solution.py:38
  23.4 0.2 reverse
  23.5 0.5 copy-done.11
  24.0 0.1 multiply_select_fusion
  24.1 0.9 collective-permute-done.2
  25.1 0.1 multiply_bitcast_fusion
  25.1 0.1 fusion.7
  25.2 0.1 fusion.8
  25.3 0.1 fusion.97
  25.4 0.1 fusion.96
  25.5 0.1 fusion.11
  25.6 0.1 fusion.90
  25.7 0.1 fusion.91
  25.8 0.1 fusion.25
  25.9 0.1 fusion.89
  26.0 0.1 fusion.88
  26.1 0.1 fusion.21
  26.2 0.1 fusion.82
  26.3 0.1 fusion.83
  26.4 0.1 fusion.37
  26.5 0.1 fusion.81
  26.6 0.1 fusion.33
  26.7 0.1 fusion.74
  26.8 0.1 fusion.75
  26.9 0.1 fusion.49
  27.0 0.1 fusion.73
  27.2 0.1 fusion.45
  27.3 0.1 fusion.67
  27.6 0.1 maximum_bitcast_fusion.3
  27.7 0.1 compare_convert_fusion
  27.8 0.1 fusion.53
  27.9 0.1 fusion.55
  28.0 0.3 compare_select_fusion
  28.3 0.3 copy-done.5
  28.6 0.3 copy-done.3
  29.0 0.3 fusion.4
  29.4 0.7 pad_maximum_fusion.7
  30.0 13.3 %shard_map.156 = f32[128,4,512]{2,1,0:T(4,128)} custom-call(f32[128,128]{1,0:T(8,128)} %bitcast.62, s32[128,1024]{1,0:T(8,128)} %bitcast.56, f32[128,1024]{1,0:T(8,128)} %bitcast.58, s32[128,1]{1,0:T(8,128)} %copy.19.tally_ref), custom_call_target="tpu_custom_call" | custom-call | tf_op jit(solution)/shard_map/pallas_call | solution.py:109
  43.3 12.7 %all-to-all-start.1 = ((f32[128,4,512]{2,1,0:T(4,128)}), f32[128,4,512]{2,1,0:T(4,128)S(1)}, u32[]{:S(2)}, u32[]{:S(2)}) async-start(f32[128,4,512]{2,1,0:T(4,128)} %shard_map.156), calls=%async_computation.1 | async-start | bytes 2097152 | tf_op jit(solution)/shard_map/all_to_all | solution.py:263
  56.0 13.4 %shard_map.155 = f32[128,4,512]{2,1,0:T(4,128)} custom-call(f32[128,128]{1,0:T(8,128)} %bitcast.63, s32[128,1024]{1,0:T(8,128)} %bitcast.57, f32[128,1024]{1,0:T(8,128)} %bitcast.59, s32[128,1]{1,0:T(8,128)} %copy.19.tally_ref), custom_call_target="tpu_custom_call" | custom-call | tf_op jit(solution)/shard_map/pallas_call | solution.py:109
  69.4 5.6 %all-to-all-done.1.value_ref = f32[128,4,512]{2,1,0:T(4,128)S(1)} async-done(((f32[128,4,512]{2,1,0:T(4,128)}), f32[128,4,512]{2,1,0:T(4,128)S(1)}, u32[]{:S(2)}, u32[]{:S(2)}) %all-to-all-start.1) | async-done | bytes 1048608 | tf_op jit(solution)/shard_map/all_to_all | solution.py:263
  75.0 1.0 copy-done
  76.0 4.3 %all-to-all-start = ((f32[128,4,512]{2,1,0:T(4,128)}), f32[128,4,512]{2,1,0:T(4,128)S(1)}, u32[]{:S(2)}, u32[]{:S(2)}) async-start(f32[128,4,512]{2,1,0:T(4,128)} %shard_map.155), calls=%async_computation | async-start | bytes 2097152 | tf_op jit(solution)/shard_map/all_to_all | solution.py:263
  80.3 0.7 slice.437
  81.0 0.7 broadcast_in_dim.2.start_ref
  81.7 11.3 %shard_map.157.start_ref = f32[256,128]{1,0:T(8,128)} custom-call(f32[128,4,512]{2,1,0:T(4,128)} %copy-done, s32[128,1024]{1,0:T(8,128)} %bitcast.60, f32[256,128]{1,0:T(8,128)} %broadcast_in_dim.2.start_ref), custom_call_target="tpu_custom_call", output_to_operand_aliasing={{}: (2, {})} | custom-call | tf_op jit(solution)/shard_map/pallas_call | solution.py:164
  93.0 6.4 %all-to-all-done.value_ref = f32[128,4,512]{2,1,0:T(4,128)S(1)} async-done(((f32[128,4,512]{2,1,0:T(4,128)}), f32[128,4,512]{2,1,0:T(4,128)S(1)}, u32[]{:S(2)}, u32[]{:S(2)}) %all-to-all-start) | async-done | bytes 1048608 | tf_op jit(solution)/shard_map/all_to_all | solution.py:263
  99.3 1.0 copy-done.1
  100.4 11.3 %shard_map.158 = f32[256,128]{1,0:T(8,128)} custom-call(f32[128,4,512]{2,1,0:T(4,128)} %copy-done.1, s32[128,1024]{1,0:T(8,128)} %bitcast.61, f32[256,128]{1,0:T(8,128)} %shard_map.157.start_ref), custom_call_target="tpu_custom_call", output_to_operand_aliasing={{}: (2, {})} | custom-call | tf_op jit(solution)/shard_map/pallas_call | solution.py:164
  111.7 0.9 reshape.41
  112.6 0.7 reduce_sum.9
  (48 shorter events, 0.7 us)
Async XLA Ops:
  0.6 0.7 copy-start.7
  1.4 0.7 copy-start.8
  2.1 0.7 copy-start.9
  3.8 7.0 %collective-permute-start = (f32[12,32,8]{2,1,0:T(8,128)S(1)}, f32[12,32,8]{2,1,0:T(8,128)S(1)}, u32[]{:S(2)}, u32[]{:S(2)}) collective-permute-start(f32[12,32,8]{2,1,0:T(8,128)S(1)} %get-tuple-element.22), channel_id=1, source_target_pairs={{0,1},{1,2},{2,3},{3,4},{4,5},{5,6},{6,7},{7,8},{8,9},{9,10},{10,1... | collective-permute-start | bytes 36872 | tf_op jit(solution)/shard_map/ppermute | solution.py:32
  8.2 7.2 %collective-permute-start.1 = (f32[12,32,8]{2,1,0:T(8,128)S(1)}, f32[12,32,8]{2,1,0:T(8,128)S(1)}, u32[]{:S(2)}, u32[]{:S(2)}) collective-permute-start(f32[12,32,8]{2,1,0:T(8,128)S(1)} %get-tuple-element.23), channel_id=1, source_target_pairs={{1,0},{2,1},{3,2},{4,3},{5,4},{6,5},{7,6},{8,7},{9,8},{10,9},{11,1... | collective-permute-start | bytes 36872 | tf_op jit(solution)/shard_map/ppermute | solution.py:33
  15.6 7.8 %collective-permute-start.3 = (f32[12,8,144]{2,1,0:T(8,128)S(1)}, f32[12,8,144]{2,1,0:T(8,128)S(1)}, u32[]{:S(2)}, u32[]{:S(2)}) collective-permute-start(f32[12,8,144]{2,1,0:T(8,128)S(1)} %get-tuple-element.20), channel_id=1, source_target_pairs={{112,127},{113,126},{114,125},{115,124},{116,123},{117,122},{118,1... | collective-permute-start | bytes 165896 | tf_op jit(solution)/shard_map/ppermute | solution.py:42
  16.2 7.3 %collective-permute-start.4 = (f32[12,8,144]{2,1,0:T(8,128)S(1)}, f32[12,8,144]{2,1,0:T(8,128)S(1)}, u32[]{:S(2)}, u32[]{:S(2)}) collective-permute-start(f32[12,8,144]{2,1,0:T(8,128)S(1)} %get-tuple-element.21), channel_id=1, source_target_pairs={{16,0},{32,16},{48,32},{64,48},{80,64},{96,80},{112,96},{17,1},{33... | collective-permute-start | bytes 165896 | tf_op jit(solution)/shard_map/ppermute | solution.py:39
  17.7 0.7 copy-start.10
  19.1 6.0 %collective-permute-start.2 = (f32[12,8,144]{2,1,0:T(8,128)S(1)}, f32[12,8,144]{2,1,0:T(8,128)S(1)}, u32[]{:S(2)}, u32[]{:S(2)}) collective-permute-start(f32[12,8,144]{2,1,0:T(8,128)S(1)} %get-tuple-element.20), channel_id=1, source_target_pairs={{0,16},{16,32},{32,48},{48,64},{64,80},{80,96},{96,112},{1,17},{17... | collective-permute-start | bytes 165896 | tf_op jit(solution)/shard_map/ppermute | solution.py:38
  23.4 0.7 copy-start.11
  28.0 0.6 copy-start.5
  28.0 0.6 copy-start.6
  28.0 0.9 copy-start.3
  28.0 1.0 copy-start.4
  29.3 14.0 %copy-start.2 = (f32[8,32,128]{2,1,0:T(8,128)}, f32[8,32,128]{2,1,0:T(8,128)S(1)}, u32[]{:S(2)}) copy-start(f32[8,32,128]{2,1,0:T(8,128)S(1)} %get-tuple-element.5) | copy-start | bytes 393220
  43.3 31.7 %all-to-all-start.1 = ((f32[128,4,512]{2,1,0:T(4,128)}), f32[128,4,512]{2,1,0:T(4,128)S(1)}, u32[]{:S(2)}, u32[]{:S(2)}) async-start(f32[128,4,512]{2,1,0:T(4,128)} %shard_map.156), calls=%async_computation.1 | async-start | bytes 2097152 | tf_op jit(solution)/shard_map/all_to_all | solution.py:263
  75.0 1.0 copy-start
  76.0 23.3 %all-to-all-start = ((f32[128,4,512]{2,1,0:T(4,128)}), f32[128,4,512]{2,1,0:T(4,128)S(1)}, u32[]{:S(2)}, u32[]{:S(2)}) async-start(f32[128,4,512]{2,1,0:T(4,128)} %shard_map.155), calls=%async_computation | async-start | bytes 2097152 | tf_op jit(solution)/shard_map/all_to_all | solution.py:263
  99.3 1.0 copy-start.1

commit v3 on v2

--- a/solution.py
+++ b/solution.py
@@ -5,6 +5,7 @@
 import jax.numpy as jnp
 from jax import lax
 from jax.experimental import pallas as pl
+from jax.experimental.pallas import tpu as pltpu
 from jax.sharding import PartitionSpec as P
 
 VERTICAL_STRATA = 8
@@ -120,19 +121,26 @@
     )(table, indices, extent, tally[:, None])
 
 
-def spread_kernel(value_ref, target_ref, start_ref, out_ref):
+def spread_kernel(has_start, final, value_ref, target_ref, *refs):
+    if has_start:
+        start_ref, refs = refs[0], refs[1:]
+    out_ref = refs[0]
+    acc_ref = refs[1] if final else out_ref
     fields_count = value_ref.shape[1]
     slots = value_ref.shape[2]
-    lows = out_ref.shape[1]
-    highs = out_ref.shape[0] // (2 * fields_count)
+    lows = acc_ref.shape[1]
+    highs = acc_ref.shape[0] // (2 * fields_count)
 
     @pl.when(pl.program_id(0) == 0)
     def _():
-        out_ref[...] = start_ref[...]
+        if has_start:
+            acc_ref[...] = start_ref[...]
+        else:
+            acc_ref[...] = jnp.zeros_like(acc_ref)
 
     high_ids = lax.broadcasted_iota(jnp.int32, (highs, slots), 0)
     low_ids = lax.broadcasted_iota(jnp.int32, (lows, slots), 0)
-    total = jnp.zeros(out_ref.shape, jnp.float32)
+    total = jnp.zeros(acc_ref.shape, jnp.float32)
     for sender in range(target_ref.shape[0]):
         target = target_ref[pl.ds(sender, 1), :]
         high_hot = high_ids == target // lows
@@ -152,27 +160,45 @@
         total = total + lax.dot_general(
             weighted, low_hot, (((1,), (1,)), ((), ())), preferred_element_type=jnp.float32
         )
-    out_ref[...] += total
+    acc_ref[...] += total
+
+    if final:
+
+        @pl.when(pl.program_id(0) == pl.num_programs(0) - 1)
+        def _():
+            half = fields_count * highs
+            for field in range(fields_count):
+                for high in range(highs):
+                    row = field * highs + high
+                    out_ref[pl.ds(field, 1), pl.ds(high * lows, lows)] = (
+                        acc_ref[pl.ds(row, 1), :] + acc_ref[pl.ds(half + row, 1), :]
+                    )
 
 
 SPREAD_LOWS = 128
 
 
-def spread_cells(values, targets, chunk, start):
+def spread_cells(values, targets, chunk, start, final):
     senders, fields_count, slots = values.shape
-    shape = start.shape
+    highs = ACELL // SPREAD_LOWS
+    shape = (2 * fields_count * highs, SPREAD_LOWS)
+    in_specs = [
+        pl.BlockSpec((GROUP, fields_count, slots), lambda i: (i, 0, 0)),
+        pl.BlockSpec((GROUP, slots), lambda i: (i, chunk)),
+    ]
+    operands = [values, targets]
+    if start is not None:
+        in_specs.append(pl.BlockSpec(shape, lambda i: (0, 0)))
+        operands.append(start)
+    out_shape = (fields_count, ACELL) if final else shape
     return pl.pallas_call(
-        spread_kernel,
-        out_shape=jax.ShapeDtypeStruct(shape, jnp.float32),
+        functools.partial(spread_kernel, start is not None, final),
+        out_shape=jax.ShapeDtypeStruct(out_shape, jnp.float32),
         grid=(senders // GROUP,),
-        in_specs=[
-            pl.BlockSpec((GROUP, fields_count, slots), lambda i: (i, 0, 0)),
-            pl.BlockSpec((GROUP, slots), lambda i: (i, chunk)),
-            pl.BlockSpec(shape, lambda i: (0, 0)),
-        ],
-        out_specs=pl.BlockSpec(shape, lambda i: (0, 0)),
-        input_output_aliases={2: 0},
-    )(values, targets, start)
+        in_specs=in_specs,
+        out_specs=pl.BlockSpec(out_shape, lambda i: (0, 0)),
+        scratch_shapes=[pltpu.VMEM(shape, jnp.float32)] if final else [],
+    )(*operands)
 
 
 def local(
@@ -249,8 +275,7 @@
     surface_grid = jnp.stack([height, speed_east[0], speed_north[0], tracer_new[0]])
     slots = sent_sender_mesh_index.shape[2]
     width = slots // CHUNKS
-    highs = ACELL // SPREAD_LOWS
-    summed = jnp.zeros((2 * NF * highs, SPREAD_LOWS), jnp.float32)
+    summed = None
     for chunk in range(CHUNKS):
         values = pick_cells(
             surface_grid,
@@ -261,8 +286,10 @@
             width,
         )
         block = lax.all_to_all(values, ("lat", "lon"), split_axis=0, concat_axis=0, tiled=True)
-        summed = spread_cells(block, received_atmosphere_mesh_index[0], chunk, summed)
-    atmosphere = summed.reshape(2, NF, ACELL).sum(axis=0)
+        summed = spread_cells(
+            block, received_atmosphere_mesh_index[0], chunk, summed, chunk == CHUNKS - 1
+        )
+    atmosphere = summed
     return (height, east, north, tracer_new, atmosphere)
 
 

time: 114 us -> 113 us (level)
  local copies, waits for them, and re-layouts: 11.7 us -> 10.1 us
where the time goes in v3:
time: 113 us; the launch traced here: 112 us
  Pallas kernels  49.2 us (44%)
  starting transfers between devices  28.3 us (25%)
  waiting for transfers between devices  20.9 us (18%)
  local copies, waits for them, and re-layouts  10.1 us (9%)
  other arithmetic  2.93 us (3%)
    pallas_call x2, Pallas kernels, pick_cells(): pl.pallas_call(functools.partial(pick_kernel, chunk * slots), out_shape=j...  26.7 us
    pallas_call x2, Pallas kernels, spread_cells(): pl.pallas_call(functools.partial(spread_kernel, start is not None, final)...  22.6 us
    all_to_all x2, starting transfers between devices, local(): lax.all_to_all(values, ('lat', 'lon'), split_axis=0, concat_axis=0, tiled...  17.7 us
    all_to_all x2, waiting for transfers between devices, local(): lax.all_to_all(values, ('lat', 'lon'), split_axis=0, concat_axis=0, tiled...  12.7 us
    unnamed x28, local copies, waits for them, and re-layouts  6.16 us
    ppermute x1, waiting for transfers between devices, exchange(): from_east = lax.ppermute(block[:, :, :width], 'lon', westward)  4.6 us
    ppermute x1, starting transfers between devices, exchange(): from_west = lax.ppermute(block[:, :, columns - width:], 'lon', eastward)  4.36 us
    ppermute x1, starting transfers between devices, exchange(): from_south = lax.ppermute(top, 'lat', upward)  4.27 us
  transfers between devices with their start and end apart: 7, of which 5 were waited for; matrix products, arithmetic and copies ran while one was open for 2% of the time, Pallas kernels for 22%

profile of v3, /device:TPU:1, one launch (start us, length us, event | category | flops | bytes accessed | tf_op | source)
XLA Modules:
  0.0 112.5 jit_solution(16138998172672648430)
XLA Ops:
  0.6 0.7 bitcast_dynamic-update-slice_fusion.3
  1.4 0.7 copy-done.8
  2.1 0.7 copy-done.9
  2.8 0.9 constant_dynamic-update-slice_fusion
  3.7 0.1 fusion.65
  3.8 4.4 %collective-permute-start = (f32[12,32,8]{2,1,0:T(8,128)S(1)}, f32[12,32,8]{2,1,0:T(8,128)S(1)}, u32[]{:S(2)}, u32[]{:S(2)}) collective-permute-start(f32[12,32,8]{2,1,0:T(8,128)S(1)} %get-tuple-element.22), channel_id=1, source_target_pairs={{0,1},{1,2},{2,3},{3,4},{4,5},{5,6},{6,7},{7,8},{8,9},{9,10},{10,1... | collective-permute-start | bytes 36872 | tf_op jit(solution)/shard_map/ppermute | solution.py:33
  8.2 2.6 %collective-permute-done = f32[12,32,8]{2,1,0:T(8,128)S(1)} collective-permute-done((f32[12,32,8]{2,1,0:T(8,128)S(1)}, f32[12,32,8]{2,1,0:T(8,128)S(1)}, u32[]{:S(2)}, u32[]{:S(2)}) %collective-permute-start) | collective-permute-done | bytes 12320 | tf_op jit(solution)/shard_map/ppermute | solution.py:33
  10.8 4.6 %collective-permute-done.1 = f32[12,32,8]{2,1,0:T(8,128)S(1)} collective-permute-done((f32[12,32,8]{2,1,0:T(8,128)S(1)}, f32[12,32,8]{2,1,0:T(8,128)S(1)}, u32[]{:S(2)}, u32[]{:S(2)}) %collective-permute-start.1) | collective-permute-done | bytes 12320 | tf_op jit(solution)/shard_map/ppermute | solution.py:34
  15.4 0.1 pad_maximum_fusion.6
  15.6 1.3 %collective-permute-start.4 = (f32[12,8,144]{2,1,0:T(8,128)S(1)}, f32[12,8,144]{2,1,0:T(8,128)S(1)}, u32[]{:S(2)}, u32[]{:S(2)}) collective-permute-start(f32[12,8,144]{2,1,0:T(8,128)S(1)} %get-tuple-element.21), channel_id=1, source_target_pairs={{16,0},{32,16},{48,32},{64,48},{80,64},{96,80},{112,96},{17,1},{33... | collective-permute-start | bytes 165896 | tf_op jit(solution)/shard_map/ppermute | solution.py:40
  16.9 0.7 collective-permute-start.3
  17.7 0.7 copy-done.10
  18.3 0.7 copy.17.tally_ref
  19.1 4.3 %collective-permute-start.2 = (f32[12,8,144]{2,1,0:T(8,128)S(1)}, f32[12,8,144]{2,1,0:T(8,128)S(1)}, u32[]{:S(2)}, u32[]{:S(2)}) collective-permute-start(f32[12,8,144]{2,1,0:T(8,128)S(1)} %get-tuple-element.20), channel_id=1, source_target_pairs={{0,16},{16,32},{32,48},{48,64},{64,80},{80,96},{96,112},{1,17},{17... | collective-permute-start | bytes 165896 | tf_op jit(solution)/shard_map/ppermute | solution.py:39
  23.4 0.2 reverse
  23.5 0.5 copy-done.11
  24.0 0.1 multiply_select_fusion
  24.1 0.9 collective-permute-done.2
  25.1 0.1 multiply_bitcast_fusion
  25.1 0.1 fusion.7
  25.2 0.1 fusion.8
  25.3 0.1 fusion.96
  25.4 0.1 fusion.97
  25.5 0.1 fusion.11
  25.6 0.1 fusion.91
  25.7 0.1 fusion.90
  25.8 0.1 fusion.25
  25.9 0.1 fusion.88
  26.0 0.1 fusion.89
  26.1 0.1 fusion.21
  26.2 0.1 fusion.83
  26.3 0.1 fusion.82
  26.4 0.1 fusion.37
  26.5 0.1 fusion.80
  26.6 0.1 fusion.81
  26.7 0.1 fusion.33
  26.8 0.1 fusion.75
  26.9 0.1 fusion.74
  26.9 0.1 fusion.49
  27.1 0.1 fusion.72
  27.1 0.1 fusion.73
  27.2 0.1 fusion.45
  27.4 0.1 fusion.66
  27.5 0.1 fusion.67
  27.6 0.1 maximum_bitcast_fusion.3
  27.7 0.1 compare_convert_fusion
  27.8 0.1 fusion.53
  27.9 0.1 fusion.55
  28.1 0.3 compare_select_fusion
  28.3 0.3 copy-done.5
  28.6 0.3 copy-done.3
  29.0 0.3 fusion.4
  29.4 0.7 pad_maximum_fusion.7
  30.1 13.3 %shard_map.156 = f32[128,4,512]{2,1,0:T(4,128)} custom-call(f32[128,128]{1,0:T(8,128)} %bitcast.62, s32[128,1024]{1,0:T(8,128)} %bitcast.56, f32[128,1024]{1,0:T(8,128)} %bitcast.58, s32[128,1]{1,0:T(8,128)} %copy.17.tally_ref), custom_call_target="tpu_custom_call" | custom-call | tf_op jit(solution)/shard_map/pallas_call | solution.py:110
  43.3 13.4 %all-to-all-start.1 = ((f32[128,4,512]{2,1,0:T(4,128)}), f32[128,4,512]{2,1,0:T(4,128)S(1)}, u32[]{:S(2)}, u32[]{:S(2)}) async-start(f32[128,4,512]{2,1,0:T(4,128)} %shard_map.156), calls=%async_computation.1 | async-start | bytes 2097152 | tf_op jit(solution)/shard_map/all_to_all | solution.py:288
  56.8 13.4 %shard_map.155 = f32[128,4,512]{2,1,0:T(4,128)} custom-call(f32[128,128]{1,0:T(8,128)} %bitcast.63, s32[128,1024]{1,0:T(8,128)} %bitcast.57, f32[128,1024]{1,0:T(8,128)} %bitcast.59, s32[128,1]{1,0:T(8,128)} %copy.17.tally_ref), custom_call_target="tpu_custom_call" | custom-call | tf_op jit(solution)/shard_map/pallas_call | solution.py:110
  70.1 5.6 %all-to-all-done.1.value_ref = f32[128,4,512]{2,1,0:T(4,128)S(1)} async-done(((f32[128,4,512]{2,1,0:T(4,128)}), f32[128,4,512]{2,1,0:T(4,128)S(1)}, u32[]{:S(2)}, u32[]{:S(2)}) %all-to-all-start.1) | async-done | bytes 1048608 | tf_op jit(solution)/shard_map/all_to_all | solution.py:288
  75.8 1.0 copy-done.1
  76.8 4.3 %all-to-all-start = ((f32[128,4,512]{2,1,0:T(4,128)}), f32[128,4,512]{2,1,0:T(4,128)S(1)}, u32[]{:S(2)}, u32[]{:S(2)}) async-start(f32[128,4,512]{2,1,0:T(4,128)} %shard_map.155), calls=%async_computation | async-start | bytes 2097152 | tf_op jit(solution)/shard_map/all_to_all | solution.py:288
  81.1 0.7 slice.437
  81.8 11.2 %shard_map.157.refs_0_ = f32[256,128]{1,0:T(8,128)} custom-call(f32[128,4,512]{2,1,0:T(4,128)} %copy-done.1, s32[128,1024]{1,0:T(8,128)} %bitcast.60), custom_call_target="tpu_custom_call" | custom-call | tf_op jit(solution)/shard_map/pallas_call | solution.py:194
  93.0 7.1 %all-to-all-done.value_ref = f32[128,4,512]{2,1,0:T(4,128)S(1)} async-done(((f32[128,4,512]{2,1,0:T(4,128)}), f32[128,4,512]{2,1,0:T(4,128)S(1)}, u32[]{:S(2)}, u32[]{:S(2)}) %all-to-all-start) | async-done | bytes 1048608 | tf_op jit(solution)/shard_map/all_to_all | solution.py:288
  100.1 1.0 copy-done
  101.1 11.3 %shard_map.158 = f32[4,4096]{1,0:T(4,128)} custom-call(f32[128,4,512]{2,1,0:T(4,128)} %copy-done, s32[128,1024]{1,0:T(8,128)} %bitcast.61, f32[256,128]{1,0:T(8,128)} %shard_map.157.refs_0_), custom_call_target="tpu_custom_call" | custom-call | tf_op jit(solution)/shard_map/pallas_call | solution.py:194
  (45 shorter events, 0.5 us)
Async XLA Ops:
  0.6 0.7 copy-start.7
  1.4 0.7 copy-start.8
  2.1 0.7 copy-start.9
  3.8 7.0 %collective-permute-start = (f32[12,32,8]{2,1,0:T(8,128)S(1)}, f32[12,32,8]{2,1,0:T(8,128)S(1)}, u32[]{:S(2)}, u32[]{:S(2)}) collective-permute-start(f32[12,32,8]{2,1,0:T(8,128)S(1)} %get-tuple-element.22), channel_id=1, source_target_pairs={{0,1},{1,2},{2,3},{3,4},{4,5},{5,6},{6,7},{7,8},{8,9},{9,10},{10,1... | collective-permute-start | bytes 36872 | tf_op jit(solution)/shard_map/ppermute | solution.py:33
  8.2 7.2 %collective-permute-start.1 = (f32[12,32,8]{2,1,0:T(8,128)S(1)}, f32[12,32,8]{2,1,0:T(8,128)S(1)}, u32[]{:S(2)}, u32[]{:S(2)}) collective-permute-start(f32[12,32,8]{2,1,0:T(8,128)S(1)} %get-tuple-element.23), channel_id=1, source_target_pairs={{1,0},{2,1},{3,2},{4,3},{5,4},{6,5},{7,6},{8,7},{9,8},{10,9},{11,1... | collective-permute-start | bytes 36872 | tf_op jit(solution)/shard_map/ppermute | solution.py:34
  15.6 8.0 %collective-permute-start.4 = (f32[12,8,144]{2,1,0:T(8,128)S(1)}, f32[12,8,144]{2,1,0:T(8,128)S(1)}, u32[]{:S(2)}, u32[]{:S(2)}) collective-permute-start(f32[12,8,144]{2,1,0:T(8,128)S(1)} %get-tuple-element.21), channel_id=1, source_target_pairs={{16,0},{32,16},{48,32},{64,48},{80,64},{96,80},{112,96},{17,1},{33... | collective-permute-start | bytes 165896 | tf_op jit(solution)/shard_map/ppermute | solution.py:40
  16.9 6.5 %collective-permute-start.3 = (f32[12,8,144]{2,1,0:T(8,128)S(1)}, f32[12,8,144]{2,1,0:T(8,128)S(1)}, u32[]{:S(2)}, u32[]{:S(2)}) collective-permute-start(f32[12,8,144]{2,1,0:T(8,128)S(1)} %get-tuple-element.20), channel_id=1, source_target_pairs={{112,127},{113,126},{114,125},{115,124},{116,123},{117,122},{118,1... | collective-permute-start | bytes 165896 | tf_op jit(solution)/shard_map/ppermute | solution.py:43
  17.7 0.7 copy-start.10
  19.1 6.0 %collective-permute-start.2 = (f32[12,8,144]{2,1,0:T(8,128)S(1)}, f32[12,8,144]{2,1,0:T(8,128)S(1)}, u32[]{:S(2)}, u32[]{:S(2)}) collective-permute-start(f32[12,8,144]{2,1,0:T(8,128)S(1)} %get-tuple-element.20), channel_id=1, source_target_pairs={{0,16},{16,32},{32,48},{48,64},{64,80},{80,96},{96,112},{1,17},{17... | collective-permute-start | bytes 165896 | tf_op jit(solution)/shard_map/ppermute | solution.py:39
  23.4 0.7 copy-start.11
  28.0 0.6 copy-start.5
  28.0 0.6 copy-start.6
  28.0 0.9 copy-start.3
  28.0 1.0 copy-start.4
  29.4 14.0 %copy-start.2 = (f32[8,32,128]{2,1,0:T(8,128)}, f32[8,32,128]{2,1,0:T(8,128)S(1)}, u32[]{:S(2)}) copy-start(f32[8,32,128]{2,1,0:T(8,128)S(1)} %get-tuple-element.5) | copy-start | bytes 393220
  43.3 32.4 %all-to-all-start.1 = ((f32[128,4,512]{2,1,0:T(4,128)}), f32[128,4,512]{2,1,0:T(4,128)S(1)}, u32[]{:S(2)}, u32[]{:S(2)}) async-start(f32[128,4,512]{2,1,0:T(4,128)} %shard_map.156), calls=%async_computation.1 | async-start | bytes 2097152 | tf_op jit(solution)/shard_map/all_to_all | solution.py:288
  75.8 1.0 copy-start.1
  76.8 23.3 %all-to-all-start = ((f32[128,4,512]{2,1,0:T(4,128)}), f32[128,4,512]{2,1,0:T(4,128)S(1)}, u32[]{:S(2)}, u32[]{:S(2)}) async-start(f32[128,4,512]{2,1,0:T(4,128)} %shard_map.155), calls=%async_computation | async-start | bytes 2097152 | tf_op jit(solution)/shard_map/all_to_all | solution.py:288
  100.1 1.0 copy-start

commit v4 on v3

--- a/solution.py
+++ b/solution.py
@@ -24,26 +24,38 @@
 HALO = 2 * STEPS
 
 
-def exchange(block, signs, width):
-    planes, rows, columns = block.shape
+def exchange(parts, signs, width):
+    planes, rows, columns = sum(part.shape[0] for part in parts), *parts[0].shape[1:]
     sectors = lax.axis_size("lon")
     bands = lax.axis_size("lat")
+
+    def gather(rows_part, columns_part):
+        return jnp.concatenate([part[:, rows_part, columns_part] for part in parts], axis=0)
+
+    everything = slice(None)
     eastward = [(i, (i + 1) % sectors) for i in range(sectors)]
     westward = [((i + 1) % sectors, i) for i in range(sectors)]
-    from_west = lax.ppermute(block[:, :, columns - width :], "lon", eastward)
-    from_east = lax.ppermute(block[:, :, :width], "lon", westward)
-    wide = jnp.concatenate([from_west, block, from_east], axis=2)
+    from_west = lax.ppermute(gather(everything, slice(columns - width, None)), "lon", eastward)
+    from_east = lax.ppermute(gather(everything, slice(0, width)), "lon", westward)
+
+    def band_rows(rows_part):
+        return jnp.concatenate(
+            [from_west[:, rows_part, :], gather(rows_part, everything), from_east[:, rows_part, :]],
+            axis=2,
+        )
+
     upward = [(b, b + 1) for b in range(bands - 1)]
     downward = [(b + 1, b) for b in range(bands - 1)]
-    top = wide[:, rows - width :, :]
+    top = band_rows(slice(rows - width, None))
     from_south = lax.ppermute(top, "lat", upward)
-    from_north = lax.ppermute(wide[:, :width, :], "lat", downward)
+    from_north = lax.ppermute(band_rows(slice(0, width)), "lat", downward)
     last = (bands - 1) * sectors
     mirror = [(last + j, last + sectors - 1 - j) for j in range(sectors)]
     folded = lax.ppermute(top, ("lat", "lon"), mirror)
     folded = jnp.flip(folded, axis=(1, 2)) * signs[:, None, None]
     on_top = lax.axis_index("lat") == bands - 1
     north_rim = jnp.where(on_top, folded, from_north)
+    wide = jnp.concatenate([from_west, jnp.concatenate(parts, axis=0), from_east], axis=2)
     return jnp.concatenate([from_south, wide, north_rim], axis=1)
 
 
@@ -218,13 +230,13 @@
     grid_rows = band_rows * lax.axis_size("lat")
     band = lax.axis_index("lat")
     depth = ocean_strata_total.astype(jnp.float32)
-    planes = jnp.concatenate(
-        [
-            jnp.stack([starting_sea_elevation, zonal_integrated_flux, meridional_integrated_flux, depth]),
-            thermal_anomaly,
-        ],
-        axis=0,
-    )
+    planes = [
+        starting_sea_elevation[None],
+        zonal_integrated_flux[None],
+        meridional_integrated_flux[None],
+        depth[None],
+        thermal_anomaly,
+    ]
     signs = jnp.array([1.0, -1.0, -1.0] + [1.0] * (1 + VERTICAL_STRATA), jnp.float32)
     ext = exchange(planes, signs, HALO)
     depth_ext = ext[3]

time: 113 us -> 114 us (level)
  waiting for transfers between devices: 20.9 us -> 14.7 us
  starting transfers between devices: 28.3 us -> 32.6 us
  local copies, waits for them, and re-layouts: 10.1 us -> 12.2 us
    ppermute x3, waiting for transfers between devices: 7.21 us -> 1.4 us  [the longest x1 1.39 us: exchange(): lax.ppermute(gather(everything, slice(columns - width, None)), 'lon', eas...]
    all_to_all x2, starting transfers between devices: 17.7 us -> 22.1 us  [local(): lax.all_to_all(values, ('lat', 'lon'), split_axis=0, concat_axis=0, tiled...]
    slice x1 -> x19, local copies, waits for them, and re-layouts: 0.11 us -> 1.45 us  [the longest x13 0.99 us: gather(): part[:, rows_part, columns_part]]
    unnamed x28 -> x48, local copies, waits for them, and re-layouts: 6.16 us -> 7.35 us
  transfers between devices with their start and end apart: 7 -> 7, of which waited for: 5 -> 4; matrix products, arithmetic and copies ran while one was open for 2% -> 3% of each run, Pallas kernels for 22% -> 22%
where the time goes in v4:
time: 114 us; the launch traced here: 113 us
  Pallas kernels  49.2 us (43%)
  starting transfers between devices  32.6 us (29%)
  waiting for transfers between devices  14.7 us (13%)
  local copies, waits for them, and re-layouts  12.2 us (11%)
  other arithmetic  3 us (3%)
  between operations  1.2 us (1%)
    pallas_call x2, Pallas kernels, pick_cells(): pl.pallas_call(functools.partial(pick_kernel, chunk * slots), out_shape=j...  26.7 us
    pallas_call x2, Pallas kernels, spread_cells(): pl.pallas_call(functools.partial(spread_kernel, start is not None, final)...  22.6 us
    all_to_all x2, starting transfers between devices, local(): lax.all_to_all(values, ('lat', 'lon'), split_axis=0, concat_axis=0, tiled...  22.1 us
    all_to_all x2, waiting for transfers between devices, local(): lax.all_to_all(values, ('lat', 'lon'), split_axis=0, concat_axis=0, tiled...  12.7 us
    unnamed x48, local copies, waits for them, and re-layouts  7.35 us
    ppermute x1, starting transfers between devices, exchange(): from_south = lax.ppermute(top, 'lat', upward)  4.16 us
    ppermute x1, starting transfers between devices, exchange(): lax.ppermute(gather(everything, slice(columns - width, None)), 'lon', eas...  2.99 us
  transfers between devices with their start and end apart: 7, of which 4 were waited for; matrix products, arithmetic and copies ran while one was open for 3% of the time, Pallas kernels for 22%

profile of v4, /device:TPU:1, one launch (start us, length us, event | category | flops | bytes accessed | tf_op | source)
XLA Modules:
  0.0 113.0 jit_solution(8217248027394269658)
XLA Ops:
  0.6 0.8 copy.19
  1.5 0.1 copy.20
  1.6 0.6 copy-done.9
  2.2 0.1 copy.21
  2.3 0.6 copy-done.10
  2.9 0.1 copy.22
  3.0 0.8 copy-done.2
  3.8 0.1 fusion.65
  3.9 0.1 copy.46
  4.0 1.5 %collective-permute-start.1 = (f32[12,32,8]{1,2,0:T(8,128)S(1)}, f32[12,32,8]{1,2,0:T(8,128)S(1)}, u32[]{:S(2)}, u32[]{:S(2)}) collective-permute-start(f32[12,32,8]{1,2,0:T(8,128)S(1)} %constant_dynamic-update-slice_fusion.10), channel_id=1, source_target_pairs={{1,0},{2,1},{3,2},{4,3},{5,4},{6,5},{7,6},{8,7},{9,8},{10,9},{11,1... | collective-permute-start | bytes 36872 | tf_op jit(solution)/shard_map/ppermute | solution.py:39
  5.5 0.1 copy.45
  5.6 3.0 %collective-permute-start = (f32[12,32,8]{1,2,0:T(8,128)S(1)}, f32[12,32,8]{1,2,0:T(8,128)S(1)}, u32[]{:S(2)}, u32[]{:S(2)}) collective-permute-start(f32[12,32,8]{1,2,0:T(8,128)S(1)} %constant_dynamic-update-slice_fusion), channel_id=1, source_target_pairs={{0,1},{1,2},{2,3},{3,4},{4,5},{5,6},{6,7},{7,8},{8,9},{9,10},{10,1... | collective-permute-start | bytes 36872 | tf_op jit(solution)/shard_map/ppermute | solution.py:38
  8.8 0.1 fusion.66
  8.9 0.1 fusion.67
  9.0 0.1 fusion.68
  9.1 0.1 fusion.69
  9.9 1.4 %collective-permute-done = f32[12,32,8]{1,2,0:T(8,128)S(1)} collective-permute-done((f32[12,32,8]{1,2,0:T(8,128)S(1)}, f32[12,32,8]{1,2,0:T(8,128)S(1)}, u32[]{:S(2)}, u32[]{:S(2)}) %collective-permute-start) | collective-permute-done | bytes 12320 | tf_op jit(solution)/shard_map/ppermute | solution.py:38
  11.4 0.1 copy.41
  11.5 0.1 fusion.103
  11.7 0.1 copy.42
  11.8 0.1 pad_maximum_fusion.5
  11.9 1.3 %collective-permute-start.4 = (f32[12,8,144]{2,1,0:T(8,128)S(1)}, f32[12,8,144]{2,1,0:T(8,128)S(1)}, u32[]{:S(2)}, u32[]{:S(2)}) collective-permute-start(f32[12,8,144]{2,1,0:T(8,128)S(1)} %pad_maximum_fusion.5), channel_id=1, source_target_pairs={{16,0},{32,16},{48,32},{64,48},{80,64},{96,80},{112,96},{17,1},{33... | collective-permute-start | bytes 165896 | tf_op jit(solution)/shard_map/ppermute | solution.py:51
  13.2 0.1 pad_maximum_fusion.4
  13.3 0.7 collective-permute-start.3
  14.1 0.7 copy-done.11
  14.8 0.7 copy.43.tally_ref
  15.5 4.2 %collective-permute-start.2 = (f32[12,8,144]{2,1,0:T(8,128)S(1)}, f32[12,8,144]{2,1,0:T(8,128)S(1)}, u32[]{:S(2)}, u32[]{:S(2)}) collective-permute-start(f32[12,8,144]{2,1,0:T(8,128)S(1)} %pad_maximum_fusion.4), channel_id=1, source_target_pairs={{0,16},{16,32},{32,48},{48,64},{64,80},{80,96},{96,112},{1,17},{17... | collective-permute-start | bytes 165896 | tf_op jit(solution)/shard_map/ppermute | solution.py:50
  19.7 0.1 copy.36
  19.8 0.1 copy.35
  19.9 0.2 reverse
  20.1 0.5 copy-done.12
  20.6 0.1 multiply_select_fusion
  20.7 0.6 collective-permute-done.2
  21.3 0.1 multiply_bitcast_fusion
  21.4 0.1 fusion.7
  21.5 0.1 fusion.8
  21.7 0.1 fusion.11
  21.9 0.1 fusion.94
  22.0 0.1 fusion.25
  22.3 0.1 fusion.21
  22.6 0.1 fusion.37
  22.9 0.1 fusion.33
  23.2 0.1 fusion.49
  23.5 0.1 fusion.45
  23.8 0.1 maximum_bitcast_fusion.3
  23.9 0.1 compare_convert_fusion
  24.0 0.1 fusion.53
  24.1 0.1 fusion.55
  24.3 0.3 compare_select_fusion
  24.6 0.3 copy-done.6
  24.9 0.3 copy-done.4
  25.2 0.3 fusion.4
  25.6 0.6 pad_maximum_fusion.6
  26.3 13.3 %shard_map.156 = f32[128,4,512]{2,1,0:T(4,128)} custom-call(f32[128,128]{1,0:T(8,128)} %bitcast.68, s32[128,1024]{1,0:T(8,128)} %bitcast.53, f32[128,1024]{1,0:T(8,128)} %bitcast.55, s32[128,1]{1,0:T(8,128)} %copy.43.tally_ref), custom_call_target="tpu_custom_call" | custom-call | tf_op jit(solution)/shard_map/pallas_call | solution.py:122
  39.6 17.7 %all-to-all-start.1 = ((f32[128,4,512]{2,1,0:T(4,128)}), f32[128,4,512]{2,1,0:T(4,128)S(1)}, u32[]{:S(2)}, u32[]{:S(2)}) async-start(f32[128,4,512]{2,1,0:T(4,128)} %shard_map.156), calls=%async_computation.1 | async-start | bytes 2097152 | tf_op jit(solution)/shard_map/all_to_all | solution.py:300
  57.3 13.4 %shard_map.155 = f32[128,4,512]{2,1,0:T(4,128)} custom-call(f32[128,128]{1,0:T(8,128)} %bitcast.69, s32[128,1024]{1,0:T(8,128)} %bitcast.54, f32[128,1024]{1,0:T(8,128)} %bitcast.56, s32[128,1]{1,0:T(8,128)} %copy.43.tally_ref), custom_call_target="tpu_custom_call" | custom-call | tf_op jit(solution)/shard_map/pallas_call | solution.py:122
  70.7 5.6 %all-to-all-done.1.value_ref = f32[128,4,512]{2,1,0:T(4,128)S(1)} async-done(((f32[128,4,512]{2,1,0:T(4,128)}), f32[128,4,512]{2,1,0:T(4,128)S(1)}, u32[]{:S(2)}, u32[]{:S(2)}) %all-to-all-start.1) | async-done | bytes 1048608 | tf_op jit(solution)/shard_map/all_to_all | solution.py:300
  76.3 1.0 copy-done.1
  77.3 4.3 %all-to-all-start = ((f32[128,4,512]{2,1,0:T(4,128)}), f32[128,4,512]{2,1,0:T(4,128)S(1)}, u32[]{:S(2)}, u32[]{:S(2)}) async-start(f32[128,4,512]{2,1,0:T(4,128)} %shard_map.155), calls=%async_computation | async-start | bytes 2097152 | tf_op jit(solution)/shard_map/all_to_all | solution.py:300
  81.6 0.7 slice.535
  82.3 11.2 %shard_map.157.refs_0_ = f32[256,128]{1,0:T(8,128)} custom-call(f32[128,4,512]{2,1,0:T(4,128)} %copy-done.1, s32[128,1024]{1,0:T(8,128)} %bitcast.57), custom_call_target="tpu_custom_call" | custom-call | tf_op jit(solution)/shard_map/pallas_call | solution.py:206
  93.5 7.1 %all-to-all-done.value_ref = f32[128,4,512]{2,1,0:T(4,128)S(1)} async-done(((f32[128,4,512]{2,1,0:T(4,128)}), f32[128,4,512]{2,1,0:T(4,128)S(1)}, u32[]{:S(2)}, u32[]{:S(2)}) %all-to-all-start) | async-done | bytes 1048608 | tf_op jit(solution)/shard_map/all_to_all | solution.py:300
  100.6 1.0 copy-done
  101.7 11.3 %shard_map.158 = f32[4,4096]{1,0:T(4,128)} custom-call(f32[128,4,512]{2,1,0:T(4,128)} %copy-done, s32[128,1024]{1,0:T(8,128)} %bitcast.58, f32[256,128]{1,0:T(8,128)} %shard_map.157.refs_0_), custom_call_target="tpu_custom_call" | custom-call | tf_op jit(solution)/shard_map/pallas_call | solution.py:206
  (93 shorter events, 2.7 us)
Async XLA Ops:
  0.6 0.8 copy-start.8
  1.5 0.7 copy-start.9
  2.2 0.7 copy-start.10
  2.9 0.9 copy-start.2
  4.0 7.5 %collective-permute-start.1 = (f32[12,32,8]{1,2,0:T(8,128)S(1)}, f32[12,32,8]{1,2,0:T(8,128)S(1)}, u32[]{:S(2)}, u32[]{:S(2)}) collective-permute-start(f32[12,32,8]{1,2,0:T(8,128)S(1)} %constant_dynamic-update-slice_fusion.10), channel_id=1, source_target_pairs={{1,0},{2,1},{3,2},{4,3},{5,4},{6,5},{7,6},{8,7},{9,8},{10,9},{11,1... | collective-permute-start | bytes 36872 | tf_op jit(solution)/shard_map/ppermute | solution.py:39
  5.6 5.7 %collective-permute-start = (f32[12,32,8]{1,2,0:T(8,128)S(1)}, f32[12,32,8]{1,2,0:T(8,128)S(1)}, u32[]{:S(2)}, u32[]{:S(2)}) collective-permute-start(f32[12,32,8]{1,2,0:T(8,128)S(1)} %constant_dynamic-update-slice_fusion), channel_id=1, source_target_pairs={{0,1},{1,2},{2,3},{3,4},{4,5},{5,6},{6,7},{7,8},{8,9},{9,10},{10,1... | collective-permute-start | bytes 36872 | tf_op jit(solution)/shard_map/ppermute | solution.py:38
  11.9 8.2 %collective-permute-start.4 = (f32[12,8,144]{2,1,0:T(8,128)S(1)}, f32[12,8,144]{2,1,0:T(8,128)S(1)}, u32[]{:S(2)}, u32[]{:S(2)}) collective-permute-start(f32[12,8,144]{2,1,0:T(8,128)S(1)} %pad_maximum_fusion.5), channel_id=1, source_target_pairs={{16,0},{32,16},{48,32},{64,48},{80,64},{96,80},{112,96},{17,1},{33... | collective-permute-start | bytes 165896 | tf_op jit(solution)/shard_map/ppermute | solution.py:51
  13.3 6.6 %collective-permute-start.3 = (f32[12,8,144]{2,1,0:T(8,128)S(1)}, f32[12,8,144]{2,1,0:T(8,128)S(1)}, u32[]{:S(2)}, u32[]{:S(2)}) collective-permute-start(f32[12,8,144]{2,1,0:T(8,128)S(1)} %pad_maximum_fusion.4), channel_id=1, source_target_pairs={{112,127},{113,126},{114,125},{115,124},{116,123},{117,122},{118,1... | collective-permute-start | bytes 165896 | tf_op jit(solution)/shard_map/ppermute | solution.py:54
  14.1 0.7 copy-start.11
  15.5 5.8 %collective-permute-start.2 = (f32[12,8,144]{2,1,0:T(8,128)S(1)}, f32[12,8,144]{2,1,0:T(8,128)S(1)}, u32[]{:S(2)}, u32[]{:S(2)}) collective-permute-start(f32[12,8,144]{2,1,0:T(8,128)S(1)} %pad_maximum_fusion.4), channel_id=1, source_target_pairs={{0,16},{16,32},{32,48},{48,64},{64,80},{80,96},{96,112},{1,17},{17... | collective-permute-start | bytes 165896 | tf_op jit(solution)/shard_map/ppermute | solution.py:50
  19.9 0.7 copy-start.12
  24.2 0.6 copy-start.6
  24.2 0.6 copy-start.7
  24.3 0.9 copy-start.4
  24.3 1.0 copy-start.5
  25.6 14.0 %copy-start.3 = (f32[8,32,128]{2,1,0:T(8,128)}, f32[8,32,128]{2,1,0:T(8,128)S(1)}, u32[]{:S(2)}) copy-start(f32[8,32,128]{2,1,0:T(8,128)S(1)} %get-tuple-element.5) | copy-start | bytes 393220
  39.6 36.8 %all-to-all-start.1 = ((f32[128,4,512]{2,1,0:T(4,128)}), f32[128,4,512]{2,1,0:T(4,128)S(1)}, u32[]{:S(2)}, u32[]{:S(2)}) async-start(f32[128,4,512]{2,1,0:T(4,128)} %shard_map.156), calls=%async_computation.1 | async-start | bytes 2097152 | tf_op jit(solution)/shard_map/all_to_all | solution.py:300
  76.3 1.0 copy-start.1
  77.3 23.3 %all-to-all-start = ((f32[128,4,512]{2,1,0:T(4,128)}), f32[128,4,512]{2,1,0:T(4,128)S(1)}, u32[]{:S(2)}, u32[]{:S(2)}) async-start(f32[128,4,512]{2,1,0:T(4,128)} %shard_map.155), calls=%async_computation | async-start | bytes 2097152 | tf_op jit(solution)/shard_map/all_to_all | solution.py:300
  100.6 1.0 copy-start

commit v5 on v3

--- a/solution.py
+++ b/solution.py
@@ -63,7 +63,7 @@
     return jnp.concatenate([x[..., :1, :], x[..., :-1, :]], axis=-2)
 
 
-GROUP = 32
+GROUP = 64
 CHUNKS = 2
 
 
@@ -145,14 +145,11 @@
         target = target_ref[pl.ds(sender, 1), :]
         high_hot = high_ids == target // lows
         low_hot = (low_ids == target % lows).astype(jnp.bfloat16)
-        pieces = []
-        for field in range(fields_count):
-            high, low_part = split_pieces(value_ref[sender, pl.ds(field, 1), :])
-            pieces.append((high, low_part))
+        pieces = [part.astype(jnp.float32) for part in split_pieces(value_ref[sender])]
         weighted = jnp.concatenate(
             [
-                jnp.where(high_hot, pieces[field][part].astype(jnp.float32), 0.0).astype(jnp.bfloat16)
-                for part in range(2)
+                jnp.where(high_hot, part[field : field + 1], 0.0).astype(jnp.bfloat16)
+                for part in pieces
                 for field in range(fields_count)
             ],
             axis=0,

time: 113 us -> 113 us (level)
  no operation moved by 1% of the time
where the time goes in v5:
time: 113 us; the launch traced here: 112 us
  Pallas kernels  48.5 us (43%)
  starting transfers between devices  28.3 us (25%)
  waiting for transfers between devices  21.3 us (19%)
  local copies, waits for them, and re-layouts  10.1 us (9%)
  other arithmetic  2.92 us (3%)
    pallas_call x2, Pallas kernels, pick_cells(): pl.pallas_call(functools.partial(pick_kernel, chunk * slots), out_shape=j...  26.7 us
    pallas_call x2, Pallas kernels, spread_cells(): pl.pallas_call(functools.partial(spread_kernel, start is not None, final)...  21.8 us
    all_to_all x2, starting transfers between devices, local(): lax.all_to_all(values, ('lat', 'lon'), split_axis=0, concat_axis=0, tiled...  17.7 us
    all_to_all x2, waiting for transfers between devices, local(): lax.all_to_all(values, ('lat', 'lon'), split_axis=0, concat_axis=0, tiled...  13.1 us
    unnamed x28, local copies, waits for them, and re-layouts  6.16 us
    ppermute x1, waiting for transfers between devices, exchange(): from_east = lax.ppermute(block[:, :, :width], 'lon', westward)  4.6 us
    ppermute x1, starting transfers between devices, exchange(): from_west = lax.ppermute(block[:, :, columns - width:], 'lon', eastward)  4.36 us
    ppermute x1, starting transfers between devices, exchange(): from_south = lax.ppermute(top, 'lat', upward)  4.27 us
  transfers between devices with their start and end apart: 7, of which 5 were waited for; matrix products, arithmetic and copies ran while one was open for 2% of the time, Pallas kernels for 22%

profile of v5, /device:TPU:1, one launch (start us, length us, event | category | flops | bytes accessed | tf_op | source)
XLA Modules:
  0.0 112.1 jit_solution(12190548229019045088)
XLA Ops:
  0.6 0.7 bitcast_dynamic-update-slice_fusion.3
  1.4 0.7 copy-done.8
  2.1 0.7 copy-done.9
  2.8 0.9 constant_dynamic-update-slice_fusion
  3.7 0.1 fusion.65
  3.8 4.4 %collective-permute-start = (f32[12,32,8]{2,1,0:T(8,128)S(1)}, f32[12,32,8]{2,1,0:T(8,128)S(1)}, u32[]{:S(2)}, u32[]{:S(2)}) collective-permute-start(f32[12,32,8]{2,1,0:T(8,128)S(1)} %get-tuple-element.22), channel_id=1, source_target_pairs={{0,1},{1,2},{2,3},{3,4},{4,5},{5,6},{6,7},{7,8},{8,9},{9,10},{10,1... | collective-permute-start | bytes 36872 | tf_op jit(solution)/shard_map/ppermute | solution.py:33
  8.2 2.6 %collective-permute-done = f32[12,32,8]{2,1,0:T(8,128)S(1)} collective-permute-done((f32[12,32,8]{2,1,0:T(8,128)S(1)}, f32[12,32,8]{2,1,0:T(8,128)S(1)}, u32[]{:S(2)}, u32[]{:S(2)}) %collective-permute-start) | collective-permute-done | bytes 12320 | tf_op jit(solution)/shard_map/ppermute | solution.py:33
  10.8 4.6 %collective-permute-done.1 = f32[12,32,8]{2,1,0:T(8,128)S(1)} collective-permute-done((f32[12,32,8]{2,1,0:T(8,128)S(1)}, f32[12,32,8]{2,1,0:T(8,128)S(1)}, u32[]{:S(2)}, u32[]{:S(2)}) %collective-permute-start.1) | collective-permute-done | bytes 12320 | tf_op jit(solution)/shard_map/ppermute | solution.py:34
  15.4 0.1 pad_maximum_fusion.6
  15.6 1.3 %collective-permute-start.4 = (f32[12,8,144]{2,1,0:T(8,128)S(1)}, f32[12,8,144]{2,1,0:T(8,128)S(1)}, u32[]{:S(2)}, u32[]{:S(2)}) collective-permute-start(f32[12,8,144]{2,1,0:T(8,128)S(1)} %get-tuple-element.21), channel_id=1, source_target_pairs={{16,0},{32,16},{48,32},{64,48},{80,64},{96,80},{112,96},{17,1},{33... | collective-permute-start | bytes 165896 | tf_op jit(solution)/shard_map/ppermute | solution.py:40
  16.9 0.7 collective-permute-start.3
  17.7 0.7 copy-done.10
  18.3 0.7 copy.17.tally_ref
  19.1 4.3 %collective-permute-start.2 = (f32[12,8,144]{2,1,0:T(8,128)S(1)}, f32[12,8,144]{2,1,0:T(8,128)S(1)}, u32[]{:S(2)}, u32[]{:S(2)}) collective-permute-start(f32[12,8,144]{2,1,0:T(8,128)S(1)} %get-tuple-element.20), channel_id=1, source_target_pairs={{0,16},{16,32},{32,48},{48,64},{64,80},{80,96},{96,112},{1,17},{17... | collective-permute-start | bytes 165896 | tf_op jit(solution)/shard_map/ppermute | solution.py:39
  23.4 0.2 reverse
  23.5 0.5 copy-done.11
  24.0 0.1 multiply_select_fusion
  24.1 0.9 collective-permute-done.2
  25.1 0.1 multiply_bitcast_fusion
  25.1 0.1 fusion.7
  25.2 0.1 fusion.8
  25.3 0.1 fusion.96
  25.4 0.1 fusion.97
  25.5 0.1 fusion.11
  25.6 0.1 fusion.91
  25.7 0.1 fusion.90
  25.8 0.1 fusion.25
  25.9 0.1 fusion.88
  26.0 0.1 fusion.89
  26.1 0.1 fusion.21
  26.2 0.1 fusion.83
  26.3 0.1 fusion.82
  26.4 0.1 fusion.37
  26.5 0.1 fusion.80
  26.6 0.1 fusion.81
  26.7 0.1 fusion.33
  26.8 0.1 fusion.75
  26.9 0.1 fusion.74
  26.9 0.1 fusion.49
  27.1 0.1 fusion.72
  27.1 0.1 fusion.73
  27.2 0.1 fusion.45
  27.4 0.1 fusion.66
  27.5 0.1 fusion.67
  27.6 0.1 maximum_bitcast_fusion.3
  27.7 0.1 compare_convert_fusion
  27.8 0.1 fusion.53
  27.9 0.1 fusion.55
  28.1 0.3 compare_select_fusion
  28.3 0.3 copy-done.5
  28.6 0.3 copy-done.3
  29.0 0.3 fusion.4
  29.4 0.6 pad_maximum_fusion.7
  30.0 13.4 %shard_map.156 = f32[128,4,512]{2,1,0:T(4,128)} custom-call(f32[128,128]{1,0:T(8,128)} %bitcast.62, s32[128,1024]{1,0:T(8,128)} %bitcast.56, f32[128,1024]{1,0:T(8,128)} %bitcast.58, s32[128,1]{1,0:T(8,128)} %copy.17.tally_ref), custom_call_target="tpu_custom_call" | custom-call | tf_op jit(solution)/shard_map/pallas_call | solution.py:110
  43.4 13.4 %all-to-all-start.1 = ((f32[128,4,512]{2,1,0:T(4,128)}), f32[128,4,512]{2,1,0:T(4,128)S(1)}, u32[]{:S(2)}, u32[]{:S(2)}) async-start(f32[128,4,512]{2,1,0:T(4,128)} %shard_map.156), calls=%async_computation.1 | async-start | bytes 2097152 | tf_op jit(solution)/shard_map/all_to_all | solution.py:285
  56.8 13.4 %shard_map.155 = f32[128,4,512]{2,1,0:T(4,128)} custom-call(f32[128,128]{1,0:T(8,128)} %bitcast.63, s32[128,1024]{1,0:T(8,128)} %bitcast.57, f32[128,1024]{1,0:T(8,128)} %bitcast.59, s32[128,1]{1,0:T(8,128)} %copy.17.tally_ref), custom_call_target="tpu_custom_call" | custom-call | tf_op jit(solution)/shard_map/pallas_call | solution.py:110
  70.2 5.6 %all-to-all-done.1.value_ref = f32[128,4,512]{2,1,0:T(4,128)S(1)} async-done(((f32[128,4,512]{2,1,0:T(4,128)}), f32[128,4,512]{2,1,0:T(4,128)S(1)}, u32[]{:S(2)}, u32[]{:S(2)}) %all-to-all-start.1) | async-done | bytes 1048608 | tf_op jit(solution)/shard_map/all_to_all | solution.py:285
  75.8 1.0 copy-done.1
  76.8 4.3 %all-to-all-start = ((f32[128,4,512]{2,1,0:T(4,128)}), f32[128,4,512]{2,1,0:T(4,128)S(1)}, u32[]{:S(2)}, u32[]{:S(2)}) async-start(f32[128,4,512]{2,1,0:T(4,128)} %shard_map.155), calls=%async_computation | async-start | bytes 2097152 | tf_op jit(solution)/shard_map/all_to_all | solution.py:285
  81.2 0.7 slice.437
  81.8 10.8 %shard_map.157.refs_0_ = f32[256,128]{1,0:T(8,128)} custom-call(f32[128,4,512]{2,1,0:T(4,128)} %copy-done.1, s32[128,1024]{1,0:T(8,128)} %bitcast.60), custom_call_target="tpu_custom_call" | custom-call | tf_op jit(solution)/shard_map/pallas_call | solution.py:191
  92.7 7.5 %all-to-all-done.value_ref = f32[128,4,512]{2,1,0:T(4,128)S(1)} async-done(((f32[128,4,512]{2,1,0:T(4,128)}), f32[128,4,512]{2,1,0:T(4,128)S(1)}, u32[]{:S(2)}, u32[]{:S(2)}) %all-to-all-start) | async-done | bytes 1048608 | tf_op jit(solution)/shard_map/all_to_all | solution.py:285
  100.2 1.0 copy-done
  101.2 10.9 %shard_map.158 = f32[4,4096]{1,0:T(4,128)} custom-call(f32[128,4,512]{2,1,0:T(4,128)} %copy-done, s32[128,1024]{1,0:T(8,128)} %bitcast.61, f32[256,128]{1,0:T(8,128)} %shard_map.157.refs_0_), custom_call_target="tpu_custom_call" | custom-call | tf_op jit(solution)/shard_map/pallas_call | solution.py:191
  (45 shorter events, 0.5 us)
Async XLA Ops:
  0.6 0.7 copy-start.7
  1.4 0.7 copy-start.8
  2.1 0.7 copy-start.9
  3.8 7.0 %collective-permute-start = (f32[12,32,8]{2,1,0:T(8,128)S(1)}, f32[12,32,8]{2,1,0:T(8,128)S(1)}, u32[]{:S(2)}, u32[]{:S(2)}) collective-permute-start(f32[12,32,8]{2,1,0:T(8,128)S(1)} %get-tuple-element.22), channel_id=1, source_target_pairs={{0,1},{1,2},{2,3},{3,4},{4,5},{5,6},{6,7},{7,8},{8,9},{9,10},{10,1... | collective-permute-start | bytes 36872 | tf_op jit(solution)/shard_map/ppermute | solution.py:33
  8.2 7.2 %collective-permute-start.1 = (f32[12,32,8]{2,1,0:T(8,128)S(1)}, f32[12,32,8]{2,1,0:T(8,128)S(1)}, u32[]{:S(2)}, u32[]{:S(2)}) collective-permute-start(f32[12,32,8]{2,1,0:T(8,128)S(1)} %get-tuple-element.23), channel_id=1, source_target_pairs={{1,0},{2,1},{3,2},{4,3},{5,4},{6,5},{7,6},{8,7},{9,8},{10,9},{11,1... | collective-permute-start | bytes 36872 | tf_op jit(solution)/shard_map/ppermute | solution.py:34
  15.6 8.0 %collective-permute-start.4 = (f32[12,8,144]{2,1,0:T(8,128)S(1)}, f32[12,8,144]{2,1,0:T(8,128)S(1)}, u32[]{:S(2)}, u32[]{:S(2)}) collective-permute-start(f32[12,8,144]{2,1,0:T(8,128)S(1)} %get-tuple-element.21), channel_id=1, source_target_pairs={{16,0},{32,16},{48,32},{64,48},{80,64},{96,80},{112,96},{17,1},{33... | collective-permute-start | bytes 165896 | tf_op jit(solution)/shard_map/ppermute | solution.py:40
  16.9 6.5 %collective-permute-start.3 = (f32[12,8,144]{2,1,0:T(8,128)S(1)}, f32[12,8,144]{2,1,0:T(8,128)S(1)}, u32[]{:S(2)}, u32[]{:S(2)}) collective-permute-start(f32[12,8,144]{2,1,0:T(8,128)S(1)} %get-tuple-element.20), channel_id=1, source_target_pairs={{112,127},{113,126},{114,125},{115,124},{116,123},{117,122},{118,1... | collective-permute-start | bytes 165896 | tf_op jit(solution)/shard_map/ppermute | solution.py:43
  17.7 0.7 copy-start.10
  19.1 6.0 %collective-permute-start.2 = (f32[12,8,144]{2,1,0:T(8,128)S(1)}, f32[12,8,144]{2,1,0:T(8,128)S(1)}, u32[]{:S(2)}, u32[]{:S(2)}) collective-permute-start(f32[12,8,144]{2,1,0:T(8,128)S(1)} %get-tuple-element.20), channel_id=1, source_target_pairs={{0,16},{16,32},{32,48},{48,64},{64,80},{80,96},{96,112},{1,17},{17... | collective-permute-start | bytes 165896 | tf_op jit(solution)/shard_map/ppermute | solution.py:39
  23.4 0.7 copy-start.11
  28.0 0.6 copy-start.5
  28.0 0.6 copy-start.6
  28.0 0.9 copy-start.3
  28.0 1.0 copy-start.4
  29.4 14.1 %copy-start.2 = (f32[8,32,128]{2,1,0:T(8,128)}, f32[8,32,128]{2,1,0:T(8,128)S(1)}, u32[]{:S(2)}) copy-start(f32[8,32,128]{2,1,0:T(8,128)S(1)} %get-tuple-element.5) | copy-start | bytes 393220
  43.4 32.4 %all-to-all-start.1 = ((f32[128,4,512]{2,1,0:T(4,128)}), f32[128,4,512]{2,1,0:T(4,128)S(1)}, u32[]{:S(2)}, u32[]{:S(2)}) async-start(f32[128,4,512]{2,1,0:T(4,128)} %shard_map.156), calls=%async_computation.1 | async-start | bytes 2097152 | tf_op jit(solution)/shard_map/all_to_all | solution.py:285
  75.8 1.0 copy-start.1
  76.8 23.3 %all-to-all-start = ((f32[128,4,512]{2,1,0:T(4,128)}), f32[128,4,512]{2,1,0:T(4,128)S(1)}, u32[]{:S(2)}, u32[]{:S(2)}) async-start(f32[128,4,512]{2,1,0:T(4,128)} %shard_map.155), calls=%async_computation | async-start | bytes 2097152 | tf_op jit(solution)/shard_map/all_to_all | solution.py:285
  100.2 1.0 copy-start

commit v6 on v5

--- a/solution.py
+++ b/solution.py
@@ -64,6 +64,7 @@
 
 
 GROUP = 64
+SPREAD_GROUP = 128
 CHUNKS = 2
 
 
@@ -180,8 +181,8 @@
     highs = ACELL // SPREAD_LOWS
     shape = (2 * fields_count * highs, SPREAD_LOWS)
     in_specs = [
-        pl.BlockSpec((GROUP, fields_count, slots), lambda i: (i, 0, 0)),
-        pl.BlockSpec((GROUP, slots), lambda i: (i, chunk)),
+        pl.BlockSpec((SPREAD_GROUP, fields_count, slots), lambda i: (i, 0, 0)),
+        pl.BlockSpec((SPREAD_GROUP, slots), lambda i: (i, chunk)),
     ]
     operands = [values, targets]
     if start is not None:
@@ -191,7 +192,7 @@
     return pl.pallas_call(
         functools.partial(spread_kernel, start is not None, final),
         out_shape=jax.ShapeDtypeStruct(out_shape, jnp.float32),
-        grid=(senders // GROUP,),
+        grid=(senders // SPREAD_GROUP,),
         in_specs=in_specs,
         out_specs=pl.BlockSpec(out_shape, lambda i: (0, 0)),
         scratch_shapes=[pltpu.VMEM(shape, jnp.float32)] if final else [],

time: 113 us -> 113 us (level)
  no operation moved by 1% of the time
where the time goes in v6:
time: 113 us; the launch traced here: 112 us
  Pallas kernels  48.8 us (43%)
  starting transfers between devices  28.5 us (25%)
  waiting for transfers between devices  21.1 us (19%)
  local copies, waits for them, and re-layouts  10.1 us (9%)
  other arithmetic  2.91 us (3%)
    pallas_call x2, Pallas kernels, pick_cells(): pl.pallas_call(functools.partial(pick_kernel, chunk * slots), out_shape=j...  26.7 us
    pallas_call x2, Pallas kernels, spread_cells(): pl.pallas_call(functools.partial(spread_kernel, start is not None, final)...  22 us
    all_to_all x2, starting transfers between devices, local(): lax.all_to_all(values, ('lat', 'lon'), split_axis=0, concat_axis=0, tiled...  17.9 us
    all_to_all x2, waiting for transfers between devices, local(): lax.all_to_all(values, ('lat', 'lon'), split_axis=0, concat_axis=0, tiled...  12.9 us
    unnamed x28, local copies, waits for them, and re-layouts  6.16 us
    ppermute x1, waiting for transfers between devices, exchange(): from_east = lax.ppermute(block[:, :, :width], 'lon', westward)  4.6 us
    ppermute x1, starting transfers between devices, exchange(): from_west = lax.ppermute(block[:, :, columns - width:], 'lon', eastward)  4.36 us
    ppermute x1, starting transfers between devices, exchange(): from_south = lax.ppermute(top, 'lat', upward)  4.27 us
  transfers between devices with their start and end apart: 7, of which 5 were waited for; matrix products, arithmetic and copies ran while one was open for 2% of the time, Pallas kernels for 22%

profile of v6, /device:TPU:1, one launch (start us, length us, event | category | flops | bytes accessed | tf_op | source)
XLA Modules:
  0.0 112.4 jit_solution(3140838515207868274)
XLA Ops:
  0.6 0.7 bitcast_dynamic-update-slice_fusion.3
  1.4 0.7 copy-done.8
  2.1 0.7 copy-done.9
  2.8 0.9 constant_dynamic-update-slice_fusion
  3.7 0.1 fusion.65
  3.8 4.4 %collective-permute-start = (f32[12,32,8]{2,1,0:T(8,128)S(1)}, f32[12,32,8]{2,1,0:T(8,128)S(1)}, u32[]{:S(2)}, u32[]{:S(2)}) collective-permute-start(f32[12,32,8]{2,1,0:T(8,128)S(1)} %get-tuple-element.22), channel_id=1, source_target_pairs={{0,1},{1,2},{2,3},{3,4},{4,5},{5,6},{6,7},{7,8},{8,9},{9,10},{10,1... | collective-permute-start | bytes 36872 | tf_op jit(solution)/shard_map/ppermute | solution.py:33
  8.2 2.6 %collective-permute-done = f32[12,32,8]{2,1,0:T(8,128)S(1)} collective-permute-done((f32[12,32,8]{2,1,0:T(8,128)S(1)}, f32[12,32,8]{2,1,0:T(8,128)S(1)}, u32[]{:S(2)}, u32[]{:S(2)}) %collective-permute-start) | collective-permute-done | bytes 12320 | tf_op jit(solution)/shard_map/ppermute | solution.py:33
  10.8 4.6 %collective-permute-done.1 = f32[12,32,8]{2,1,0:T(8,128)S(1)} collective-permute-done((f32[12,32,8]{2,1,0:T(8,128)S(1)}, f32[12,32,8]{2,1,0:T(8,128)S(1)}, u32[]{:S(2)}, u32[]{:S(2)}) %collective-permute-start.1) | collective-permute-done | bytes 12320 | tf_op jit(solution)/shard_map/ppermute | solution.py:34
  15.4 0.1 pad_maximum_fusion.6
  15.6 1.3 %collective-permute-start.4 = (f32[12,8,144]{2,1,0:T(8,128)S(1)}, f32[12,8,144]{2,1,0:T(8,128)S(1)}, u32[]{:S(2)}, u32[]{:S(2)}) collective-permute-start(f32[12,8,144]{2,1,0:T(8,128)S(1)} %get-tuple-element.21), channel_id=1, source_target_pairs={{16,0},{32,16},{48,32},{64,48},{80,64},{96,80},{112,96},{17,1},{33... | collective-permute-start | bytes 165896 | tf_op jit(solution)/shard_map/ppermute | solution.py:40
  16.9 0.7 collective-permute-start.3
  17.7 0.7 copy-done.10
  18.3 0.7 copy.17.tally_ref
  19.1 4.3 %collective-permute-start.2 = (f32[12,8,144]{2,1,0:T(8,128)S(1)}, f32[12,8,144]{2,1,0:T(8,128)S(1)}, u32[]{:S(2)}, u32[]{:S(2)}) collective-permute-start(f32[12,8,144]{2,1,0:T(8,128)S(1)} %get-tuple-element.20), channel_id=1, source_target_pairs={{0,16},{16,32},{32,48},{48,64},{64,80},{80,96},{96,112},{1,17},{17... | collective-permute-start | bytes 165896 | tf_op jit(solution)/shard_map/ppermute | solution.py:39
  23.4 0.2 reverse
  23.5 0.5 copy-done.11
  24.0 0.1 multiply_select_fusion
  24.1 0.9 collective-permute-done.2
  25.1 0.1 multiply_bitcast_fusion
  25.1 0.1 fusion.7
  25.2 0.1 fusion.8
  25.3 0.1 fusion.96
  25.4 0.1 fusion.97
  25.5 0.1 fusion.11
  25.6 0.1 fusion.91
  25.7 0.1 fusion.90
  25.8 0.1 fusion.25
  25.9 0.1 fusion.88
  26.0 0.1 fusion.89
  26.1 0.1 fusion.21
  26.2 0.1 fusion.83
  26.3 0.1 fusion.82
  26.4 0.1 fusion.37
  26.5 0.1 fusion.80
  26.6 0.1 fusion.81
  26.7 0.1 fusion.33
  26.8 0.1 fusion.75
  26.9 0.1 fusion.74
  26.9 0.1 fusion.49
  27.1 0.1 fusion.72
  27.1 0.1 fusion.73
  27.2 0.1 fusion.45
  27.4 0.1 fusion.66
  27.5 0.1 fusion.67
  27.6 0.1 maximum_bitcast_fusion.3
  27.7 0.1 compare_convert_fusion
  27.8 0.1 fusion.53
  27.9 0.1 fusion.55
  28.1 0.3 compare_select_fusion
  28.3 0.3 copy-done.5
  28.6 0.3 copy-done.3
  29.0 0.3 fusion.4
  29.4 0.6 pad_maximum_fusion.7
  30.0 13.4 %shard_map.156 = f32[128,4,512]{2,1,0:T(4,128)} custom-call(f32[128,128]{1,0:T(8,128)} %bitcast.62, s32[128,1024]{1,0:T(8,128)} %bitcast.56, f32[128,1024]{1,0:T(8,128)} %bitcast.58, s32[128,1]{1,0:T(8,128)} %copy.17.tally_ref), custom_call_target="tpu_custom_call" | custom-call | tf_op jit(solution)/shard_map/pallas_call | solution.py:111
  43.4 13.4 %all-to-all-start.1 = ((f32[128,4,512]{2,1,0:T(4,128)}), f32[128,4,512]{2,1,0:T(4,128)S(1)}, u32[]{:S(2)}, u32[]{:S(2)}) async-start(f32[128,4,512]{2,1,0:T(4,128)} %shard_map.156), calls=%async_computation.1 | async-start | bytes 2097152 | tf_op jit(solution)/shard_map/all_to_all | solution.py:286
  56.8 13.4 %shard_map.155 = f32[128,4,512]{2,1,0:T(4,128)} custom-call(f32[128,128]{1,0:T(8,128)} %bitcast.63, s32[128,1024]{1,0:T(8,128)} %bitcast.57, f32[128,1024]{1,0:T(8,128)} %bitcast.59, s32[128,1]{1,0:T(8,128)} %copy.17.tally_ref), custom_call_target="tpu_custom_call" | custom-call | tf_op jit(solution)/shard_map/pallas_call | solution.py:111
  70.2 5.6 %all-to-all-done.1.value_ref = f32[128,4,512]{2,1,0:T(4,128)S(1)} async-done(((f32[128,4,512]{2,1,0:T(4,128)}), f32[128,4,512]{2,1,0:T(4,128)S(1)}, u32[]{:S(2)}, u32[]{:S(2)}) %all-to-all-start.1) | async-done | bytes 1048608 | tf_op jit(solution)/shard_map/all_to_all | solution.py:286
  75.8 1.0 copy-done.1
  76.8 4.5 %all-to-all-start = ((f32[128,4,512]{2,1,0:T(4,128)}), f32[128,4,512]{2,1,0:T(4,128)S(1)}, u32[]{:S(2)}, u32[]{:S(2)}) async-start(f32[128,4,512]{2,1,0:T(4,128)} %shard_map.155), calls=%async_computation | async-start | bytes 2097152 | tf_op jit(solution)/shard_map/all_to_all | solution.py:286
  81.4 0.7 slice.437
  82.1 10.8 %shard_map.157.refs_0_ = f32[256,128]{1,0:T(8,128)} custom-call(f32[128,4,512]{2,1,0:T(4,128)} %copy-done.1, s32[128,1024]{1,0:T(8,128)} %bitcast.60), custom_call_target="tpu_custom_call" | custom-call | tf_op jit(solution)/shard_map/pallas_call | solution.py:192
  92.9 7.3 %all-to-all-done.value_ref = f32[128,4,512]{2,1,0:T(4,128)S(1)} async-done(((f32[128,4,512]{2,1,0:T(4,128)}), f32[128,4,512]{2,1,0:T(4,128)S(1)}, u32[]{:S(2)}, u32[]{:S(2)}) %all-to-all-start) | async-done | bytes 1048608 | tf_op jit(solution)/shard_map/all_to_all | solution.py:286
  100.2 1.0 copy-done
  101.2 11.2 %shard_map.158 = f32[4,4096]{1,0:T(4,128)} custom-call(f32[128,4,512]{2,1,0:T(4,128)} %copy-done, s32[128,1024]{1,0:T(8,128)} %bitcast.61, f32[256,128]{1,0:T(8,128)} %shard_map.157.refs_0_), custom_call_target="tpu_custom_call" | custom-call | tf_op jit(solution)/shard_map/pallas_call | solution.py:192
  (45 shorter events, 0.5 us)
Async XLA Ops:
  0.6 0.7 copy-start.7
  1.4 0.7 copy-start.8
  2.1 0.7 copy-start.9
  3.8 7.0 %collective-permute-start = (f32[12,32,8]{2,1,0:T(8,128)S(1)}, f32[12,32,8]{2,1,0:T(8,128)S(1)}, u32[]{:S(2)}, u32[]{:S(2)}) collective-permute-start(f32[12,32,8]{2,1,0:T(8,128)S(1)} %get-tuple-element.22), channel_id=1, source_target_pairs={{0,1},{1,2},{2,3},{3,4},{4,5},{5,6},{6,7},{7,8},{8,9},{9,10},{10,1... | collective-permute-start | bytes 36872 | tf_op jit(solution)/shard_map/ppermute | solution.py:33
  8.2 7.2 %collective-permute-start.1 = (f32[12,32,8]{2,1,0:T(8,128)S(1)}, f32[12,32,8]{2,1,0:T(8,128)S(1)}, u32[]{:S(2)}, u32[]{:S(2)}) collective-permute-start(f32[12,32,8]{2,1,0:T(8,128)S(1)} %get-tuple-element.23), channel_id=1, source_target_pairs={{1,0},{2,1},{3,2},{4,3},{5,4},{6,5},{7,6},{8,7},{9,8},{10,9},{11,1... | collective-permute-start | bytes 36872 | tf_op jit(solution)/shard_map/ppermute | solution.py:34
  15.6 8.0 %collective-permute-start.4 = (f32[12,8,144]{2,1,0:T(8,128)S(1)}, f32[12,8,144]{2,1,0:T(8,128)S(1)}, u32[]{:S(2)}, u32[]{:S(2)}) collective-permute-start(f32[12,8,144]{2,1,0:T(8,128)S(1)} %get-tuple-element.21), channel_id=1, source_target_pairs={{16,0},{32,16},{48,32},{64,48},{80,64},{96,80},{112,96},{17,1},{33... | collective-permute-start | bytes 165896 | tf_op jit(solution)/shard_map/ppermute | solution.py:40
  16.9 6.5 %collective-permute-start.3 = (f32[12,8,144]{2,1,0:T(8,128)S(1)}, f32[12,8,144]{2,1,0:T(8,128)S(1)}, u32[]{:S(2)}, u32[]{:S(2)}) collective-permute-start(f32[12,8,144]{2,1,0:T(8,128)S(1)} %get-tuple-element.20), channel_id=1, source_target_pairs={{112,127},{113,126},{114,125},{115,124},{116,123},{117,122},{118,1... | collective-permute-start | bytes 165896 | tf_op jit(solution)/shard_map/ppermute | solution.py:43
  17.7 0.7 copy-start.10
  19.1 6.0 %collective-permute-start.2 = (f32[12,8,144]{2,1,0:T(8,128)S(1)}, f32[12,8,144]{2,1,0:T(8,128)S(1)}, u32[]{:S(2)}, u32[]{:S(2)}) collective-permute-start(f32[12,8,144]{2,1,0:T(8,128)S(1)} %get-tuple-element.20), channel_id=1, source_target_pairs={{0,16},{16,32},{32,48},{48,64},{64,80},{80,96},{96,112},{1,17},{17... | collective-permute-start | bytes 165896 | tf_op jit(solution)/shard_map/ppermute | solution.py:39
  23.4 0.7 copy-start.11
  28.0 0.6 copy-start.5
  28.0 0.6 copy-start.6
  28.0 0.9 copy-start.3
  28.0 1.0 copy-start.4
  29.4 14.1 %copy-start.2 = (f32[8,32,128]{2,1,0:T(8,128)}, f32[8,32,128]{2,1,0:T(8,128)S(1)}, u32[]{:S(2)}) copy-start(f32[8,32,128]{2,1,0:T(8,128)S(1)} %get-tuple-element.5) | copy-start | bytes 393220
  43.4 32.4 %all-to-all-start.1 = ((f32[128,4,512]{2,1,0:T(4,128)}), f32[128,4,512]{2,1,0:T(4,128)S(1)}, u32[]{:S(2)}, u32[]{:S(2)}) async-start(f32[128,4,512]{2,1,0:T(4,128)} %shard_map.156), calls=%async_computation.1 | async-start | bytes 2097152 | tf_op jit(solution)/shard_map/all_to_all | solution.py:286
  75.8 1.0 copy-start.1
  76.8 23.3 %all-to-all-start = ((f32[128,4,512]{2,1,0:T(4,128)}), f32[128,4,512]{2,1,0:T(4,128)S(1)}, u32[]{:S(2)}, u32[]{:S(2)}) async-start(f32[128,4,512]{2,1,0:T(4,128)} %shard_map.155), calls=%async_computation | async-start | bytes 2097152 | tf_op jit(solution)/shard_map/all_to_all | solution.py:286
  100.2 1.0 copy-start

commit v7 on v5

--- a/solution.py
+++ b/solution.py
@@ -82,18 +82,20 @@
     table = jnp.concatenate(split_pieces(table_ref[...]), axis=1)
     column_ids = lax.broadcasted_iota(jnp.int32, (columns, slots), 0)
     row_ids = lax.broadcasted_iota(jnp.int32, (8, slots), 0)
-    slot_ids = lax.broadcasted_iota(jnp.int32, (1, slots), 1) + offset
-    for owner in range(index_ref.shape[0]):
-        index = index_ref[pl.ds(owner, 1), :]
-        hot = (column_ids == index % columns).astype(jnp.bfloat16)
+    owners = index_ref.shape[0]
+    slot_ids = lax.broadcasted_iota(jnp.int32, (owners, slots), 1) + offset
+    indices = index_ref[...]
+    column_all = indices % columns
+    row_all = indices // columns
+    weight_all = jnp.where(slot_ids < tally_ref[...], extent_ref[...], 0.0)
+    for owner in range(owners):
+        hot = (column_ids == column_all[owner : owner + 1]).astype(jnp.bfloat16)
         by_column = jnp.dot(
             table, jnp.concatenate([hot, hot], axis=0), preferred_element_type=jnp.float32
         )
-        row = index // columns
+        row = row_all[owner : owner + 1]
         masks = [row_ids + 8 * tile == row for tile in range(rows // 8)]
-        weight = jnp.where(
-            slot_ids < tally_ref[pl.ds(owner, 1), :], extent_ref[pl.ds(owner, 1), :], 0.0
-        )
+        weight = weight_all[owner : owner + 1]
         for field in range(fields_count):
             chosen = jnp.zeros((8, slots), jnp.float32)
             for tile in range(rows // 8):

time: 113 us -> 112 us (level)
  transfers between devices with their start and end apart: 7 -> 7, of which waited for: 5 -> 5; matrix products, arithmetic and copies ran while one was open for 2% -> 2% of each run, Pallas kernels for 22% -> 21%
where the time goes in v7:
time: 112 us
  Pallas kernels  47.4 us (42%)
  starting transfers between devices  28.3 us (25%)
  waiting for transfers between devices  21.8 us (19%)
  local copies, waits for them, and re-layouts  10.1 us (9%)
  other arithmetic  2.92 us (3%)
    pallas_call x2, Pallas kernels, pick_cells(): pl.pallas_call(functools.partial(pick_kernel, chunk * slots), out_shape=j...  25.7 us
    pallas_call x2, Pallas kernels, spread_cells(): pl.pallas_call(functools.partial(spread_kernel, start is not None, final)...  21.8 us
    all_to_all x2, starting transfers between devices, local(): lax.all_to_all(values, ('lat', 'lon'), split_axis=0, concat_axis=0, tiled...  17.7 us
    all_to_all x2, waiting for transfers between devices, local(): lax.all_to_all(values, ('lat', 'lon'), split_axis=0, concat_axis=0, tiled...  13.7 us
    unnamed x28, local copies, waits for them, and re-layouts  6.16 us
    ppermute x1, waiting for transfers between devices, exchange(): from_east = lax.ppermute(block[:, :, :width], 'lon', westward)  4.6 us
    ppermute x1, starting transfers between devices, exchange(): from_west = lax.ppermute(block[:, :, columns - width:], 'lon', eastward)  4.36 us
    ppermute x1, starting transfers between devices, exchange(): from_south = lax.ppermute(top, 'lat', upward)  4.27 us
  transfers between devices with their start and end apart: 7, of which 5 were waited for; matrix products, arithmetic and copies ran while one was open for 2% of the time, Pallas kernels for 21%

profile of v7, /device:TPU:1, one launch (start us, length us, event | category | flops | bytes accessed | tf_op | source)
XLA Modules:
  0.0 111.6 jit_solution(16763315595194052650)
XLA Ops:
  0.6 0.7 bitcast_dynamic-update-slice_fusion.3
  1.4 0.7 copy-done.8
  2.1 0.7 copy-done.9
  2.8 0.9 constant_dynamic-update-slice_fusion
  3.7 0.1 fusion.65
  3.8 4.4 %collective-permute-start = (f32[12,32,8]{2,1,0:T(8,128)S(1)}, f32[12,32,8]{2,1,0:T(8,128)S(1)}, u32[]{:S(2)}, u32[]{:S(2)}) collective-permute-start(f32[12,32,8]{2,1,0:T(8,128)S(1)} %get-tuple-element.22), channel_id=1, source_target_pairs={{0,1},{1,2},{2,3},{3,4},{4,5},{5,6},{6,7},{7,8},{8,9},{9,10},{10,1... | collective-permute-start | bytes 36872 | tf_op jit(solution)/shard_map/ppermute | solution.py:33
  8.2 2.6 %collective-permute-done = f32[12,32,8]{2,1,0:T(8,128)S(1)} collective-permute-done((f32[12,32,8]{2,1,0:T(8,128)S(1)}, f32[12,32,8]{2,1,0:T(8,128)S(1)}, u32[]{:S(2)}, u32[]{:S(2)}) %collective-permute-start) | collective-permute-done | bytes 12320 | tf_op jit(solution)/shard_map/ppermute | solution.py:33
  10.8 4.6 %collective-permute-done.1 = f32[12,32,8]{2,1,0:T(8,128)S(1)} collective-permute-done((f32[12,32,8]{2,1,0:T(8,128)S(1)}, f32[12,32,8]{2,1,0:T(8,128)S(1)}, u32[]{:S(2)}, u32[]{:S(2)}) %collective-permute-start.1) | collective-permute-done | bytes 12320 | tf_op jit(solution)/shard_map/ppermute | solution.py:34
  15.4 0.1 pad_maximum_fusion.6
  15.6 1.3 %collective-permute-start.4 = (f32[12,8,144]{2,1,0:T(8,128)S(1)}, f32[12,8,144]{2,1,0:T(8,128)S(1)}, u32[]{:S(2)}, u32[]{:S(2)}) collective-permute-start(f32[12,8,144]{2,1,0:T(8,128)S(1)} %get-tuple-element.21), channel_id=1, source_target_pairs={{16,0},{32,16},{48,32},{64,48},{80,64},{96,80},{112,96},{17,1},{33... | collective-permute-start | bytes 165896 | tf_op jit(solution)/shard_map/ppermute | solution.py:40
  16.9 0.7 collective-permute-start.3
  17.7 0.7 copy-done.10
  18.3 0.7 copy.17.tally_ref
  19.1 4.3 %collective-permute-start.2 = (f32[12,8,144]{2,1,0:T(8,128)S(1)}, f32[12,8,144]{2,1,0:T(8,128)S(1)}, u32[]{:S(2)}, u32[]{:S(2)}) collective-permute-start(f32[12,8,144]{2,1,0:T(8,128)S(1)} %get-tuple-element.20), channel_id=1, source_target_pairs={{0,16},{16,32},{32,48},{48,64},{64,80},{80,96},{96,112},{1,17},{17... | collective-permute-start | bytes 165896 | tf_op jit(solution)/shard_map/ppermute | solution.py:39
  23.4 0.2 reverse
  23.5 0.5 copy-done.11
  24.0 0.1 multiply_select_fusion
  24.1 0.9 collective-permute-done.2
  25.1 0.1 multiply_bitcast_fusion
  25.1 0.1 fusion.7
  25.2 0.1 fusion.8
  25.3 0.1 fusion.96
  25.4 0.1 fusion.97
  25.5 0.1 fusion.11
  25.6 0.1 fusion.91
  25.7 0.1 fusion.90
  25.8 0.1 fusion.25
  25.9 0.1 fusion.88
  26.0 0.1 fusion.89
  26.1 0.1 fusion.21
  26.2 0.1 fusion.83
  26.3 0.1 fusion.82
  26.4 0.1 fusion.37
  26.5 0.1 fusion.80
  26.6 0.1 fusion.81
  26.7 0.1 fusion.33
  26.8 0.1 fusion.75
  26.9 0.1 fusion.74
  26.9 0.1 fusion.49
  27.1 0.1 fusion.72
  27.1 0.1 fusion.73
  27.2 0.1 fusion.45
  27.4 0.1 fusion.66
  27.5 0.1 fusion.67
  27.6 0.1 maximum_bitcast_fusion.3
  27.7 0.1 compare_convert_fusion
  27.8 0.1 fusion.53
  27.9 0.1 fusion.55
  28.1 0.3 compare_select_fusion
  28.3 0.3 copy-done.5
  28.6 0.3 copy-done.3
  29.0 0.3 fusion.4
  29.4 0.6 pad_maximum_fusion.7
  30.0 12.8 %shard_map.156 = f32[128,4,512]{2,1,0:T(4,128)} custom-call(f32[128,128]{1,0:T(8,128)} %bitcast.62, s32[128,1024]{1,0:T(8,128)} %bitcast.56, f32[128,1024]{1,0:T(8,128)} %bitcast.58, s32[128,1]{1,0:T(8,128)} %copy.17.tally_ref), custom_call_target="tpu_custom_call" | custom-call | tf_op jit(solution)/shard_map/pallas_call | solution.py:112
  42.9 13.4 %all-to-all-start.1 = ((f32[128,4,512]{2,1,0:T(4,128)}), f32[128,4,512]{2,1,0:T(4,128)S(1)}, u32[]{:S(2)}, u32[]{:S(2)}) async-start(f32[128,4,512]{2,1,0:T(4,128)} %shard_map.156), calls=%async_computation.1 | async-start | bytes 2097152 | tf_op jit(solution)/shard_map/all_to_all | solution.py:287
  56.3 12.8 %shard_map.155 = f32[128,4,512]{2,1,0:T(4,128)} custom-call(f32[128,128]{1,0:T(8,128)} %bitcast.63, s32[128,1024]{1,0:T(8,128)} %bitcast.57, f32[128,1024]{1,0:T(8,128)} %bitcast.59, s32[128,1]{1,0:T(8,128)} %copy.17.tally_ref), custom_call_target="tpu_custom_call" | custom-call | tf_op jit(solution)/shard_map/pallas_call | solution.py:112
  69.1 6.2 %all-to-all-done.1.value_ref = f32[128,4,512]{2,1,0:T(4,128)S(1)} async-done(((f32[128,4,512]{2,1,0:T(4,128)}), f32[128,4,512]{2,1,0:T(4,128)S(1)}, u32[]{:S(2)}, u32[]{:S(2)}) %all-to-all-start.1) | async-done | bytes 1048608 | tf_op jit(solution)/shard_map/all_to_all | solution.py:287
  75.3 1.0 copy-done.1
  76.3 4.3 %all-to-all-start = ((f32[128,4,512]{2,1,0:T(4,128)}), f32[128,4,512]{2,1,0:T(4,128)S(1)}, u32[]{:S(2)}, u32[]{:S(2)}) async-start(f32[128,4,512]{2,1,0:T(4,128)} %shard_map.155), calls=%async_computation | async-start | bytes 2097152 | tf_op jit(solution)/shard_map/all_to_all | solution.py:287
  80.6 0.7 slice.437
  81.3 10.8 %shard_map.157.refs_0_ = f32[256,128]{1,0:T(8,128)} custom-call(f32[128,4,512]{2,1,0:T(4,128)} %copy-done.1, s32[128,1024]{1,0:T(8,128)} %bitcast.60), custom_call_target="tpu_custom_call" | custom-call | tf_op jit(solution)/shard_map/pallas_call | solution.py:193
  92.2 7.5 %all-to-all-done.value_ref = f32[128,4,512]{2,1,0:T(4,128)S(1)} async-done(((f32[128,4,512]{2,1,0:T(4,128)}), f32[128,4,512]{2,1,0:T(4,128)S(1)}, u32[]{:S(2)}, u32[]{:S(2)}) %all-to-all-start) | async-done | bytes 1048608 | tf_op jit(solution)/shard_map/all_to_all | solution.py:287
  99.7 1.0 copy-done
  100.7 10.9 %shard_map.158 = f32[4,4096]{1,0:T(4,128)} custom-call(f32[128,4,512]{2,1,0:T(4,128)} %copy-done, s32[128,1024]{1,0:T(8,128)} %bitcast.61, f32[256,128]{1,0:T(8,128)} %shard_map.157.refs_0_), custom_call_target="tpu_custom_call" | custom-call | tf_op jit(solution)/shard_map/pallas_call | solution.py:193
  (45 shorter events, 0.5 us)
Async XLA Ops:
  0.6 0.7 copy-start.7
  1.4 0.7 copy-start.8
  2.1 0.7 copy-start.9
  3.8 7.0 %collective-permute-start = (f32[12,32,8]{2,1,0:T(8,128)S(1)}, f32[12,32,8]{2,1,0:T(8,128)S(1)}, u32[]{:S(2)}, u32[]{:S(2)}) collective-permute-start(f32[12,32,8]{2,1,0:T(8,128)S(1)} %get-tuple-element.22), channel_id=1, source_target_pairs={{0,1},{1,2},{2,3},{3,4},{4,5},{5,6},{6,7},{7,8},{8,9},{9,10},{10,1... | collective-permute-start | bytes 36872 | tf_op jit(solution)/shard_map/ppermute | solution.py:33
  8.2 7.2 %collective-permute-start.1 = (f32[12,32,8]{2,1,0:T(8,128)S(1)}, f32[12,32,8]{2,1,0:T(8,128)S(1)}, u32[]{:S(2)}, u32[]{:S(2)}) collective-permute-start(f32[12,32,8]{2,1,0:T(8,128)S(1)} %get-tuple-element.23), channel_id=1, source_target_pairs={{1,0},{2,1},{3,2},{4,3},{5,4},{6,5},{7,6},{8,7},{9,8},{10,9},{11,1... | collective-permute-start | bytes 36872 | tf_op jit(solution)/shard_map/ppermute | solution.py:34
  15.6 8.0 %collective-permute-start.4 = (f32[12,8,144]{2,1,0:T(8,128)S(1)}, f32[12,8,144]{2,1,0:T(8,128)S(1)}, u32[]{:S(2)}, u32[]{:S(2)}) collective-permute-start(f32[12,8,144]{2,1,0:T(8,128)S(1)} %get-tuple-element.21), channel_id=1, source_target_pairs={{16,0},{32,16},{48,32},{64,48},{80,64},{96,80},{112,96},{17,1},{33... | collective-permute-start | bytes 165896 | tf_op jit(solution)/shard_map/ppermute | solution.py:40
  16.9 6.5 %collective-permute-start.3 = (f32[12,8,144]{2,1,0:T(8,128)S(1)}, f32[12,8,144]{2,1,0:T(8,128)S(1)}, u32[]{:S(2)}, u32[]{:S(2)}) collective-permute-start(f32[12,8,144]{2,1,0:T(8,128)S(1)} %get-tuple-element.20), channel_id=1, source_target_pairs={{112,127},{113,126},{114,125},{115,124},{116,123},{117,122},{118,1... | collective-permute-start | bytes 165896 | tf_op jit(solution)/shard_map/ppermute | solution.py:43
  17.7 0.7 copy-start.10
  19.1 6.0 %collective-permute-start.2 = (f32[12,8,144]{2,1,0:T(8,128)S(1)}, f32[12,8,144]{2,1,0:T(8,128)S(1)}, u32[]{:S(2)}, u32[]{:S(2)}) collective-permute-start(f32[12,8,144]{2,1,0:T(8,128)S(1)} %get-tuple-element.20), channel_id=1, source_target_pairs={{0,16},{16,32},{32,48},{48,64},{64,80},{80,96},{96,112},{1,17},{17... | collective-permute-start | bytes 165896 | tf_op jit(solution)/shard_map/ppermute | solution.py:39
  23.4 0.7 copy-start.11
  28.0 0.6 copy-start.5
  28.0 0.6 copy-start.6
  28.0 0.9 copy-start.3
  28.0 1.0 copy-start.4
  29.4 13.5 %copy-start.2 = (f32[8,32,128]{2,1,0:T(8,128)}, f32[8,32,128]{2,1,0:T(8,128)S(1)}, u32[]{:S(2)}) copy-start(f32[8,32,128]{2,1,0:T(8,128)S(1)} %get-tuple-element.5) | copy-start | bytes 393220
  42.9 32.4 %all-to-all-start.1 = ((f32[128,4,512]{2,1,0:T(4,128)}), f32[128,4,512]{2,1,0:T(4,128)S(1)}, u32[]{:S(2)}, u32[]{:S(2)}) async-start(f32[128,4,512]{2,1,0:T(4,128)} %shard_map.156), calls=%async_computation.1 | async-start | bytes 2097152 | tf_op jit(solution)/shard_map/all_to_all | solution.py:287
  75.3 1.0 copy-start.1
  76.3 23.3 %all-to-all-start = ((f32[128,4,512]{2,1,0:T(4,128)}), f32[128,4,512]{2,1,0:T(4,128)S(1)}, u32[]{:S(2)}, u32[]{:S(2)}) async-start(f32[128,4,512]{2,1,0:T(4,128)} %shard_map.155), calls=%async_computation | async-start | bytes 2097152 | tf_op jit(solution)/shard_map/all_to_all | solution.py:287
  99.6 1.0 copy-start

commit v8 on v7

--- a/solution.py
+++ b/solution.py
@@ -143,10 +143,12 @@
     high_ids = lax.broadcasted_iota(jnp.int32, (highs, slots), 0)
     low_ids = lax.broadcasted_iota(jnp.int32, (lows, slots), 0)
     total = jnp.zeros(acc_ref.shape, jnp.float32)
+    targets = target_ref[...]
+    high_all = targets // lows
+    low_all = targets % lows
     for sender in range(target_ref.shape[0]):
-        target = target_ref[pl.ds(sender, 1), :]
-        high_hot = high_ids == target // lows
-        low_hot = (low_ids == target % lows).astype(jnp.bfloat16)
+        high_hot = high_ids == high_all[sender : sender + 1]
+        low_hot = (low_ids == low_all[sender : sender + 1]).astype(jnp.bfloat16)
         pieces = [part.astype(jnp.float32) for part in split_pieces(value_ref[sender])]
         weighted = jnp.concatenate(
             [

time: 112 us -> 112 us (level)
  no operation moved by 1% of the time
where the time goes in v8:
time: 112 us
  Pallas kernels  47.6 us (42%)
  starting transfers between devices  28.3 us (25%)
  waiting for transfers between devices  21.8 us (19%)
  local copies, waits for them, and re-layouts  10.1 us (9%)
  other arithmetic  2.92 us (3%)
    pallas_call x2, Pallas kernels, pick_cells(): pl.pallas_call(functools.partial(pick_kernel, chunk * slots), out_shape=j...  25.7 us
    pallas_call x2, Pallas kernels, spread_cells(): pl.pallas_call(functools.partial(spread_kernel, start is not None, final)...  21.9 us
    all_to_all x2, starting transfers between devices, local(): lax.all_to_all(values, ('lat', 'lon'), split_axis=0, concat_axis=0, tiled...  17.7 us
    all_to_all x2, waiting for transfers between devices, local(): lax.all_to_all(values, ('lat', 'lon'), split_axis=0, concat_axis=0, tiled...  13.6 us
    unnamed x28, local copies, waits for them, and re-layouts  6.16 us
    ppermute x1, waiting for transfers between devices, exchange(): from_east = lax.ppermute(block[:, :, :width], 'lon', westward)  4.6 us
    ppermute x1, starting transfers between devices, exchange(): from_west = lax.ppermute(block[:, :, columns - width:], 'lon', eastward)  4.36 us
    ppermute x1, starting transfers between devices, exchange(): from_south = lax.ppermute(top, 'lat', upward)  4.27 us
  transfers between devices with their start and end apart: 7, of which 5 were waited for; matrix products, arithmetic and copies ran while one was open for 2% of the time, Pallas kernels for 21%

profile of v8, /device:TPU:1, one launch (start us, length us, event | category | flops | bytes accessed | tf_op | source)
XLA Modules:
  0.0 111.7 jit_solution(4636142616017991270)
XLA Ops:
  0.6 0.7 bitcast_dynamic-update-slice_fusion.3
  1.4 0.7 copy-done.8
  2.1 0.7 copy-done.9
  2.8 0.9 constant_dynamic-update-slice_fusion
  3.7 0.1 fusion.65
  3.8 4.4 %collective-permute-start = (f32[12,32,8]{2,1,0:T(8,128)S(1)}, f32[12,32,8]{2,1,0:T(8,128)S(1)}, u32[]{:S(2)}, u32[]{:S(2)}) collective-permute-start(f32[12,32,8]{2,1,0:T(8,128)S(1)} %get-tuple-element.22), channel_id=1, source_target_pairs={{0,1},{1,2},{2,3},{3,4},{4,5},{5,6},{6,7},{7,8},{8,9},{9,10},{10,1... | collective-permute-start | bytes 36872 | tf_op jit(solution)/shard_map/ppermute | solution.py:33
  8.2 2.6 %collective-permute-done = f32[12,32,8]{2,1,0:T(8,128)S(1)} collective-permute-done((f32[12,32,8]{2,1,0:T(8,128)S(1)}, f32[12,32,8]{2,1,0:T(8,128)S(1)}, u32[]{:S(2)}, u32[]{:S(2)}) %collective-permute-start) | collective-permute-done | bytes 12320 | tf_op jit(solution)/shard_map/ppermute | solution.py:33
  10.8 4.6 %collective-permute-done.1 = f32[12,32,8]{2,1,0:T(8,128)S(1)} collective-permute-done((f32[12,32,8]{2,1,0:T(8,128)S(1)}, f32[12,32,8]{2,1,0:T(8,128)S(1)}, u32[]{:S(2)}, u32[]{:S(2)}) %collective-permute-start.1) | collective-permute-done | bytes 12320 | tf_op jit(solution)/shard_map/ppermute | solution.py:34
  15.4 0.1 pad_maximum_fusion.6
  15.6 1.3 %collective-permute-start.4 = (f32[12,8,144]{2,1,0:T(8,128)S(1)}, f32[12,8,144]{2,1,0:T(8,128)S(1)}, u32[]{:S(2)}, u32[]{:S(2)}) collective-permute-start(f32[12,8,144]{2,1,0:T(8,128)S(1)} %get-tuple-element.21), channel_id=1, source_target_pairs={{16,0},{32,16},{48,32},{64,48},{80,64},{96,80},{112,96},{17,1},{33... | collective-permute-start | bytes 165896 | tf_op jit(solution)/shard_map/ppermute | solution.py:40
  16.9 0.7 collective-permute-start.3
  17.7 0.7 copy-done.10
  18.3 0.7 copy.17.tally_ref
  19.1 4.3 %collective-permute-start.2 = (f32[12,8,144]{2,1,0:T(8,128)S(1)}, f32[12,8,144]{2,1,0:T(8,128)S(1)}, u32[]{:S(2)}, u32[]{:S(2)}) collective-permute-start(f32[12,8,144]{2,1,0:T(8,128)S(1)} %get-tuple-element.20), channel_id=1, source_target_pairs={{0,16},{16,32},{32,48},{48,64},{64,80},{80,96},{96,112},{1,17},{17... | collective-permute-start | bytes 165896 | tf_op jit(solution)/shard_map/ppermute | solution.py:39
  23.4 0.2 reverse
  23.5 0.5 copy-done.11
  24.0 0.1 multiply_select_fusion
  24.1 0.9 collective-permute-done.2
  25.1 0.1 multiply_bitcast_fusion
  25.1 0.1 fusion.7
  25.2 0.1 fusion.8
  25.3 0.1 fusion.96
  25.4 0.1 fusion.97
  25.5 0.1 fusion.11
  25.6 0.1 fusion.91
  25.7 0.1 fusion.90
  25.8 0.1 fusion.25
  25.9 0.1 fusion.88
  26.0 0.1 fusion.89
  26.1 0.1 fusion.21
  26.2 0.1 fusion.83
  26.3 0.1 fusion.82
  26.4 0.1 fusion.37
  26.5 0.1 fusion.80
  26.6 0.1 fusion.81
  26.7 0.1 fusion.33
  26.8 0.1 fusion.75
  26.9 0.1 fusion.74
  26.9 0.1 fusion.49
  27.1 0.1 fusion.72
  27.1 0.1 fusion.73
  27.2 0.1 fusion.45
  27.4 0.1 fusion.66
  27.5 0.1 fusion.67
  27.6 0.1 maximum_bitcast_fusion.3
  27.7 0.1 compare_convert_fusion
  27.8 0.1 fusion.53
  27.9 0.1 fusion.55
  28.1 0.3 compare_select_fusion
  28.3 0.3 copy-done.5
  28.6 0.3 copy-done.3
  29.0 0.3 fusion.4
  29.4 0.6 pad_maximum_fusion.7
  30.0 12.8 %shard_map.156 = f32[128,4,512]{2,1,0:T(4,128)} custom-call(f32[128,128]{1,0:T(8,128)} %bitcast.62, s32[128,1024]{1,0:T(8,128)} %bitcast.56, f32[128,1024]{1,0:T(8,128)} %bitcast.58, s32[128,1]{1,0:T(8,128)} %copy.17.tally_ref), custom_call_target="tpu_custom_call" | custom-call | tf_op jit(solution)/shard_map/pallas_call | solution.py:112
  42.9 13.4 %all-to-all-start.1 = ((f32[128,4,512]{2,1,0:T(4,128)}), f32[128,4,512]{2,1,0:T(4,128)S(1)}, u32[]{:S(2)}, u32[]{:S(2)}) async-start(f32[128,4,512]{2,1,0:T(4,128)} %shard_map.156), calls=%async_computation.1 | async-start | bytes 2097152 | tf_op jit(solution)/shard_map/all_to_all | solution.py:289
  56.3 12.8 %shard_map.155 = f32[128,4,512]{2,1,0:T(4,128)} custom-call(f32[128,128]{1,0:T(8,128)} %bitcast.63, s32[128,1024]{1,0:T(8,128)} %bitcast.57, f32[128,1024]{1,0:T(8,128)} %bitcast.59, s32[128,1]{1,0:T(8,128)} %copy.17.tally_ref), custom_call_target="tpu_custom_call" | custom-call | tf_op jit(solution)/shard_map/pallas_call | solution.py:112
  69.1 6.2 %all-to-all-done.1.value_ref = f32[128,4,512]{2,1,0:T(4,128)S(1)} async-done(((f32[128,4,512]{2,1,0:T(4,128)}), f32[128,4,512]{2,1,0:T(4,128)S(1)}, u32[]{:S(2)}, u32[]{:S(2)}) %all-to-all-start.1) | async-done | bytes 1048608 | tf_op jit(solution)/shard_map/all_to_all | solution.py:289
  75.3 1.0 copy-done.1
  76.3 4.3 %all-to-all-start = ((f32[128,4,512]{2,1,0:T(4,128)}), f32[128,4,512]{2,1,0:T(4,128)S(1)}, u32[]{:S(2)}, u32[]{:S(2)}) async-start(f32[128,4,512]{2,1,0:T(4,128)} %shard_map.155), calls=%async_computation | async-start | bytes 2097152 | tf_op jit(solution)/shard_map/all_to_all | solution.py:289
  80.6 0.7 slice.437
  81.3 10.9 %shard_map.157.refs_0_ = f32[256,128]{1,0:T(8,128)} custom-call(f32[128,4,512]{2,1,0:T(4,128)} %copy-done.1, s32[128,1024]{1,0:T(8,128)} %bitcast.60), custom_call_target="tpu_custom_call" | custom-call | tf_op jit(solution)/shard_map/pallas_call | solution.py:195
  92.2 7.4 %all-to-all-done.value_ref = f32[128,4,512]{2,1,0:T(4,128)S(1)} async-done(((f32[128,4,512]{2,1,0:T(4,128)}), f32[128,4,512]{2,1,0:T(4,128)S(1)}, u32[]{:S(2)}, u32[]{:S(2)}) %all-to-all-start) | async-done | bytes 1048608 | tf_op jit(solution)/shard_map/all_to_all | solution.py:289
  99.7 1.0 copy-done
  100.7 11.0 %shard_map.158 = f32[4,4096]{1,0:T(4,128)} custom-call(f32[128,4,512]{2,1,0:T(4,128)} %copy-done, s32[128,1024]{1,0:T(8,128)} %bitcast.61, f32[256,128]{1,0:T(8,128)} %shard_map.157.refs_0_), custom_call_target="tpu_custom_call" | custom-call | tf_op jit(solution)/shard_map/pallas_call | solution.py:195
  (45 shorter events, 0.5 us)
Async XLA Ops:
  0.6 0.7 copy-start.7
  1.4 0.7 copy-start.8
  2.1 0.7 copy-start.9
  3.8 7.0 %collective-permute-start = (f32[12,32,8]{2,1,0:T(8,128)S(1)}, f32[12,32,8]{2,1,0:T(8,128)S(1)}, u32[]{:S(2)}, u32[]{:S(2)}) collective-permute-start(f32[12,32,8]{2,1,0:T(8,128)S(1)} %get-tuple-element.22), channel_id=1, source_target_pairs={{0,1},{1,2},{2,3},{3,4},{4,5},{5,6},{6,7},{7,8},{8,9},{9,10},{10,1... | collective-permute-start | bytes 36872 | tf_op jit(solution)/shard_map/ppermute | solution.py:33
  8.2 7.2 %collective-permute-start.1 = (f32[12,32,8]{2,1,0:T(8,128)S(1)}, f32[12,32,8]{2,1,0:T(8,128)S(1)}, u32[]{:S(2)}, u32[]{:S(2)}) collective-permute-start(f32[12,32,8]{2,1,0:T(8,128)S(1)} %get-tuple-element.23), channel_id=1, source_target_pairs={{1,0},{2,1},{3,2},{4,3},{5,4},{6,5},{7,6},{8,7},{9,8},{10,9},{11,1... | collective-permute-start | bytes 36872 | tf_op jit(solution)/shard_map/ppermute | solution.py:34
  15.6 8.0 %collective-permute-start.4 = (f32[12,8,144]{2,1,0:T(8,128)S(1)}, f32[12,8,144]{2,1,0:T(8,128)S(1)}, u32[]{:S(2)}, u32[]{:S(2)}) collective-permute-start(f32[12,8,144]{2,1,0:T(8,128)S(1)} %get-tuple-element.21), channel_id=1, source_target_pairs={{16,0},{32,16},{48,32},{64,48},{80,64},{96,80},{112,96},{17,1},{33... | collective-permute-start | bytes 165896 | tf_op jit(solution)/shard_map/ppermute | solution.py:40
  16.9 6.5 %collective-permute-start.3 = (f32[12,8,144]{2,1,0:T(8,128)S(1)}, f32[12,8,144]{2,1,0:T(8,128)S(1)}, u32[]{:S(2)}, u32[]{:S(2)}) collective-permute-start(f32[12,8,144]{2,1,0:T(8,128)S(1)} %get-tuple-element.20), channel_id=1, source_target_pairs={{112,127},{113,126},{114,125},{115,124},{116,123},{117,122},{118,1... | collective-permute-start | bytes 165896 | tf_op jit(solution)/shard_map/ppermute | solution.py:43
  17.7 0.7 copy-start.10
  19.1 6.0 %collective-permute-start.2 = (f32[12,8,144]{2,1,0:T(8,128)S(1)}, f32[12,8,144]{2,1,0:T(8,128)S(1)}, u32[]{:S(2)}, u32[]{:S(2)}) collective-permute-start(f32[12,8,144]{2,1,0:T(8,128)S(1)} %get-tuple-element.20), channel_id=1, source_target_pairs={{0,16},{16,32},{32,48},{48,64},{64,80},{80,96},{96,112},{1,17},{17... | collective-permute-start | bytes 165896 | tf_op jit(solution)/shard_map/ppermute | solution.py:39
  23.4 0.7 copy-start.11
  28.0 0.6 copy-start.5
  28.0 0.6 copy-start.6
  28.0 0.9 copy-start.3
  28.0 1.0 copy-start.4
  29.4 13.5 %copy-start.2 = (f32[8,32,128]{2,1,0:T(8,128)}, f32[8,32,128]{2,1,0:T(8,128)S(1)}, u32[]{:S(2)}) copy-start(f32[8,32,128]{2,1,0:T(8,128)S(1)} %get-tuple-element.5) | copy-start | bytes 393220
  42.9 32.4 %all-to-all-start.1 = ((f32[128,4,512]{2,1,0:T(4,128)}), f32[128,4,512]{2,1,0:T(4,128)S(1)}, u32[]{:S(2)}, u32[]{:S(2)}) async-start(f32[128,4,512]{2,1,0:T(4,128)} %shard_map.156), calls=%async_computation.1 | async-start | bytes 2097152 | tf_op jit(solution)/shard_map/all_to_all | solution.py:289
  75.3 1.0 copy-start.1
  76.3 23.3 %all-to-all-start = ((f32[128,4,512]{2,1,0:T(4,128)}), f32[128,4,512]{2,1,0:T(4,128)S(1)}, u32[]{:S(2)}, u32[]{:S(2)}) async-start(f32[128,4,512]{2,1,0:T(4,128)} %shard_map.155), calls=%async_computation | async-start | bytes 2097152 | tf_op jit(solution)/shard_map/all_to_all | solution.py:289
  99.6 1.0 copy-start
